TPU v7x, 256 devices: a whole 4x4x8 slice. The times are simulated.
256 devices in a mesh: dp: 8 (over x, z_lo), seq: 32 (over z_hi, y, core).
Axes of the slice: x: 4, y: 4, z: 8 (z_hi: 4, z_lo: 2; z = z_hi * 2 + z_lo), core: 2. Of those that a mesh axis runs over, the one named last changes fastest.
Arguments:
- inputs: float32 [8, 4096, 2048], P('dp', 'seq'), may hold values from -6 to 6
- cotangent: float32 [8, 4096, 2048], P('dp', 'seq'), may hold values from -6 to 6
- block_mix: float32 [128, 128], replicated, may hold values from -0.5 to 0.5
- twist_hi: float32 [2, 2, 2048], replicated, may hold values from -3 to 3
- twist_lo: float32 [2, 2, 2048], replicated, may hold values from -3 to 3
- gain: float32 [2048], replicated, may hold values from 0.5 to 1.5
- gate_up: float32 [128, 2, 16, 256], P('seq'), may hold values from -0.5 to 0.5
- down: float32 [256, 16, 128], P('seq'), may hold values from -0.375 to 0.375
Outputs:
- grad_inputs: float32 [8, 4096, 2048], P('dp', 'seq')
- grad_gate_up: float32 [128, 2, 16, 256], P('seq')
- grad_down: float32 [256, 16, 128], P('seq')
- grad_block_mix: float32 [128, 128], replicated
- grad_twist_hi: float32 [2, 2, 2048], replicated
- grad_twist_lo: float32 [2, 2, 2048], replicated
- grad_gain: float32 [2048], replicated
All inputs are finite; a program needn't handle non-finite values.
Results may differ from a plain program's by a relative error of at most 0.00022.
Values sent between devices are 32-bit elements; how exact they have to be, the bound alone decides.
No kernel may reach another device: no remote copies, remote signals or barrier semaphores. Data moves between devices by JAX's collectives and lax.ppermute only.
A program may use at most 64 MiB of HBM per device.

v0:
```python
import math

import jax
import jax.numpy as jnp
from jax import lax
from jax.sharding import Mesh, PartitionSpec as P

NB = 16
BLK = 128
DB = 128


HIGH = lax.Precision.HIGH
EPS = 1e-05


def axis_count(axis):
    if isinstance(axis, tuple):
        return math.prod(lax.axis_size(a) for a in axis)
    return lax.axis_size(axis)


def from_partner(block, axis, distance):
    count = axis_count(axis)
    route = []
    for low in range(count):
        high = low | 1 << distance
        if high != low and high < count:
            route += [(low, high), (high, low)]
    return lax.ppermute(block, axis, route)


SEQ = ("zh", "loc")


def side_of(bit):
    return lax.axis_index(SEQ) // (1 << bit) % 2


def forward_section(field, coeff, bit):
    partner = from_partner(field, SEQ, bit)
    own = coeff[side_of(bit)]
    return (own[0] * field + own[1] * partner, partner)


def backward_section(grad, field, partner, coeff, bit):
    side = side_of(bit)
    own = coeff[side]
    sent = from_partner(own[1] * grad, SEQ, bit)
    back = own[0] * grad + sent
    term = jnp.stack([jnp.sum(grad * field, axis=0), jnp.sum(grad * partner, axis=0)])
    pick = (jnp.arange(2) == side).astype(jnp.float32)
    return (back, pick[:, None, None] * term[None])


def psum_doubling(x, axis):
    for bit in range(axis_count(axis).bit_length() - 1):
        x = x + from_partner(x, axis, bit)
    return x


def exchange(x, axis=SEQ):
    return lax.all_to_all(x, axis, 0, 0, tiled=True)


def per_device(inputs, cotangent, block_mix, twist_hi, twist_lo, gain, gate_up, down):
    seq_in = inputs[0]
    tokens, width = seq_in.shape
    count = axis_count(SEQ)
    group = lax.axis_size("loc")
    zcount = count // group
    nb = NB // group
    top_bit = count.bit_length() - 2
    nblocks = tokens // BLK
    rows_gu = gate_up.shape[0]
    rows_dn = down.shape[0]
    fb = gate_up.shape[3]
    size_gu = rows_gu * 2 * nb * fb

    gu_l = jnp.transpose(gate_up.reshape(rows_gu, 2, group, nb, fb), (2, 0, 1, 3, 4)).reshape(group, -1)
    dn_l = jnp.transpose(down.reshape(rows_dn, group, nb, DB), (1, 0, 2, 3)).reshape(group, -1)
    wbuf = jnp.concatenate([gu_l, dn_l], axis=1)
    wbuf = jnp.broadcast_to(wbuf[None], (zcount,) + wbuf.shape).reshape(count, -1)
    wrecv = exchange(wbuf)
    w_gu = wrecv[:, :size_gu].reshape(count * rows_gu, 2, nb, fb)
    w_dn = wrecv[:, size_gu:].reshape(count * rows_dn, nb, DB)

    def to_group(field):
        x = field.reshape(tokens, group, nb, DB)
        x = jnp.transpose(x, (1, 0, 2, 3))
        return exchange(x, "loc").reshape(group * tokens, nb, DB)

    def from_group(x):
        x = exchange(x.reshape(group, tokens, nb, DB), "loc")
        return jnp.transpose(x, (1, 0, 2, 3)).reshape(tokens, width)

    grad_out = cotangent[0]
    cot_blk = to_group(grad_out)

    xb = seq_in.reshape(nblocks, BLK, width)
    xb_peer = from_partner(xb, SEQ, top_bit)
    mixed = jnp.einsum("ij,kjd->kid", block_mix, xb, precision=HIGH).reshape(tokens, width)
    mixed_peer = jnp.einsum("ij,kjd->kid", block_mix, xb_peer, precision=HIGH).reshape(tokens, width)
    own_hi = twist_hi[side_of(top_bit)]
    first = own_hi[0] * mixed + own_hi[1] * mixed_peer
    second, first_peer = forward_section(first, twist_lo, 0)
    resid = seq_in + second
    scale = lax.rsqrt(jnp.mean(resid * resid, axis=-1, keepdims=True) + EPS)
    unit = resid * scale
    normed = unit * gain
    x_blk = to_group(normed)

    gate_val = jnp.einsum("tnd,dnf->tnf", x_blk, w_gu[:, 0], precision=HIGH)
    up_val = jnp.einsum("tnd,dnf->tnf", x_blk, w_gu[:, 1], precision=HIGH)
    sig = jax.nn.sigmoid(gate_val)
    act = gate_val * sig
    hidden = act * up_val
    grad_hidden = jnp.einsum("tnd,fnd->tnf", cot_blk, w_dn, precision=HIGH)
    grad_gate = grad_hidden * up_val * sig * (1.0 + gate_val * (1.0 - sig))
    grad_up = grad_hidden * act
    grad_x = jnp.einsum("tnf,dnf->tnd", grad_gate, w_gu[:, 0], precision=HIGH) + jnp.einsum(
        "tnf,dnf->tnd", grad_up, w_gu[:, 1], precision=HIGH
    )
    grad_normed = from_group(grad_x)

    d_gate = jnp.einsum("tnd,tnf->dnf", x_blk, grad_gate, precision=HIGH)
    d_up = jnp.einsum("tnd,tnf->dnf", x_blk, grad_up, precision=HIGH)
    d_gu = jnp.stack([d_gate, d_up], axis=1).reshape(count, -1)
    d_dn = jnp.einsum("tnf,tnd->fnd", hidden, cot_blk, precision=HIGH).reshape(count, -1)
    grecv = exchange(jnp.concatenate([d_gu, d_dn], axis=1))
    grecv = grecv.reshape(zcount, group, -1).sum(axis=0)
    part_gu = jnp.transpose(grecv[:, :size_gu].reshape(group, rows_gu, 2, nb, fb), (1, 2, 0, 3, 4))
    part_gu = part_gu.reshape(rows_gu, 2, NB, fb)
    part_down = jnp.transpose(grecv[:, size_gu:].reshape(group, rows_dn, nb, DB), (1, 0, 2, 3))
    part_down = part_down.reshape(rows_dn, NB, DB)
    n_gu = part_gu.size
    wsum = psum_doubling(jnp.concatenate([part_gu.reshape(-1), part_down.reshape(-1)]), "dp")
    part_gu = wsum[:n_gu].reshape(part_gu.shape)
    part_down = wsum[n_gu:].reshape(part_down.shape)

    grad_gain_local = jnp.sum(grad_normed * unit, axis=0)
    weighted = grad_normed * gain
    inner = jnp.mean(weighted * resid, axis=-1, keepdims=True)
    grad_resid = grad_out + scale * weighted - resid * scale * scale * scale * inner
    grad_first, term_lo = backward_section(grad_resid, first, first_peer, twist_lo, 0)
    grad_mixed, term_hi = backward_section(grad_first, mixed, mixed_peer, twist_hi, top_bit)
    grad_mb = grad_mixed.reshape(nblocks, BLK, width)
    keep = (own_hi[0] * grad_first).reshape(nblocks, BLK, width)
    give = (own_hi[1] * grad_first).reshape(nblocks, BLK, width)
    term_block = jnp.einsum("kid,kjd->ij", keep, xb, precision=HIGH) + jnp.einsum(
        "kid,kjd->ij", give, xb_peer, precision=HIGH
    )
    grad_seq = jnp.einsum("ij,kid->kjd", block_mix, grad_mb, precision=HIGH).reshape(tokens, width)
    grad_seq = grad_seq + grad_resid
    smalls = (term_block, term_hi, term_lo, grad_gain_local)
    sbuf = jnp.concatenate([t.reshape(-1) for t in smalls])
    spart = exchange(sbuf.reshape(count, -1)).sum(axis=0)
    spart = psum_doubling(spart, "dp")
    sfull = exchange(jnp.broadcast_to(spart[None], (count, spart.shape[0]))).reshape(-1)
    sums = []
    at = 0
    for t in smalls:
        sums.append(sfull[at : at + t.size].reshape(t.shape))
        at += t.size
    sum_block, sum_hi, sum_lo, sum_gain = sums
    factor = 1.0 / math.sqrt(lax.axis_size("dp") * count * tokens)
    return (
        grad_seq[None],
        part_gu * factor,
        part_down * factor,
        sum_block * factor,
        sum_hi * factor,
        sum_lo * factor,
        sum_gain * factor,
    )


def solution(mesh):
    dp_size, seq_size = mesh.devices.shape
    group = min(seq_size, NB // 2)
    split = Mesh(mesh.devices.reshape(dp_size, seq_size // group, group), ("dp",) + SEQ)
    return jax.shard_map(
        per_device,
        mesh=split,
        in_specs=(
            P("dp", SEQ, None),
            P("dp", SEQ, None),
            P(),
            P(),
            P(),
            P(),
            P(SEQ, None, None, None),
            P(SEQ, None, None),
        ),
        out_specs=(
            P("dp", SEQ, None),
            P(SEQ, None, None, None),
            P(SEQ, None, None),
            P(),
            P(),
            P(),
            P(),
        ),
        check_vma=False,
    )
```

profile of v0, /device:TPU:1, one launch (start us, length us, event | category | flops | bytes accessed | tf_op | source)
XLA Modules:
  0.0 275.3 jit_solution(5164963080848564090)
XLA Ops:
  0.6 7.8 %collective-permute-start = (f32[1,128,2048]{2,1,0:T(8,128)}, f32[1,128,2048]{2,1,0:T(8,128)S(1)}, u32[]{:S(2)}, u32[]{:S(2)}) collective-permute-start(f32[1,128,2048]{2,1,0:T(8,128)} %param.8), channel_id=1, source_target_pairs={{0,16},{16,0},{1,17},{17,1},{2,18},{18,2},{3,19},{19,3},{4,20},{20... | collective-permute-start | bytes 3145736 | tf_op jit(solution)/shard_map/ppermute | solution.py:30
  8.5 1.5 copy.125
  11.1 1.3 copy.131
  12.4 5.6 %all-to-all-start.1 = ((f32[8,128,2,128]{3,1,2,0:T(8,128)}), f32[8,128,2,128]{3,1,2,0:T(8,128)S(1)}, u32[]{:S(2)}, u32[]{:S(2)}) async-start(f32[8,128,2,128]{3,1,2,0:T(8,128)} %copy.131), calls=%async_computation.1 | async-start | bytes 2097152 | tf_op jit(solution)/shard_map/all_to_all | solution.py:63
  20.2 16.8 %collective-permute-done = f32[1,128,2048]{2,1,0:T(8,128)S(1)} collective-permute-done((f32[1,128,2048]{2,1,0:T(8,128)}, f32[1,128,2048]{2,1,0:T(8,128)S(1)}, u32[]{:S(2)}, u32[]{:S(2)}) %collective-permute-start) | collective-permute-done | bytes 1048608 | tf_op jit(solution)/shard_map/ppermute | solution.py:30
  38.0 3.2 %multiply_add_fusion.1 = (f32[128,2048]{0,1:T(8,128)S(1)}, f32[128,2048]{0,1:T(8,128)}) fusion(f32[128,2048]{0,1:T(8,128)S(1)} %convolution_bitcast_fusion.2, f32[2048]{0:T(1024)S(1)} %bitcast.209, f32[2048]{0:T(1024)S(1)} %bitcast.204, f32[128,128]{1,0:T(8,128)S(1)} %copy-done, f32[1,128,2048]{2,1,0:T(8,128)} %copy-done.11), kind=kOutput, calls=%fused_computation.45 | convolution fusion | flops 202113024 | bytes 4276224 | tf_op jit(solution)/shard_map/ij,kjd->kid/dot_general | solution.py:103
  41.2 17.1 %collective-permute-start.1 = (f32[128,2048]{0,1:T(8,128)S(1)}, f32[128,2048]{0,1:T(8,128)}, u32[]{:S(2)}, u32[]{:S(2)}) collective-permute-start(f32[128,2048]{0,1:T(8,128)S(1)} %get-tuple-element.74), channel_id=1, source_target_pairs={{0,1},{1,0},{2,3},{3,2},{4,5},{5,4},{6,7},{7,6},{8,9},{9,8},{10,11... | collective-permute-start | bytes 3145736 | tf_op jit(solution)/shard_map/ppermute | solution.py:30
  59.3 3.0 %all_to_all.33 = f32[32,1,6144]{2,1,0:T(1,128)} reshape(f32[4,8,6144]{2,1,0:T(8,128)} %broadcast_in_dim.6) | data formatting | bytes 1572864 | tf_op jit(solution)/shard_map/all_to_all | solution.py:63
  62.3 10.6 %all-to-all-start = ((f32[32,1,6144]{2,1,0:T(1,128)}), f32[32,1,6144]{2,1,0:T(1,128)}, u32[]{:S(2)}, u32[]{:S(2)}) async-start(f32[32,1,6144]{2,1,0:T(1,128)} %all_to_all.33), calls=%async_computation | async-start | bytes 1572864 | tf_op jit(solution)/shard_map/all_to_all | solution.py:63
  72.8 1.3 copy.126
  74.2 1.9 multiply_reduce_fusion.5
  76.2 1.4 multiply_multiply_fusion
  77.6 15.3 %all-to-all-done = f32[32,1,6144]{2,1,0:T(1,128)} async-done(((f32[32,1,6144]{2,1,0:T(1,128)}), f32[32,1,6144]{2,1,0:T(1,128)}, u32[]{:S(2)}, u32[]{:S(2)}) %all-to-all-start) | async-done | bytes 786464 | tf_op jit(solution)/shard_map/all_to_all | solution.py:63
  92.9 8.1 %all-to-all-start.2 = ((f32[8,128,2,128]{1,3,2,0:T(8,128)}), f32[8,128,2,128]{1,3,2,0:T(8,128)}, u32[]{:S(2)}, u32[]{:S(2)}) async-start(f32[8,128,2,128]{1,3,2,0:T(8,128)} %bitcast.23), calls=%async_computation.2 | async-start | bytes 2097152 | tf_op jit(solution)/shard_map/all_to_all | solution.py:63
  103.2 1.4 copy.169
  105.5 2.4 reshape.193
  108.8 1.9 fusion.35
  110.7 1.8 copy.155
  113.3 3.3 %fusion.31 = f32[2,256,1024]{2,1,0:T(8,128)} fusion(f32[1024,2,128]{2,0,1:T(8,128)S(1)} %bitcast.190, f32[256,2,128]{2,1,0:T(2,128)} %reshape.194), kind=kOutput, calls=%fused_computation.64 | convolution fusion | flops 402653184 | bytes 3407872 | tf_op jit(solution)/shard_map/tnd,fnd->tnf/dot_general | solution.py:118
  116.7 1.6 copy.135
  119.8 1.7 fusion.6
  121.6 2.2 fusion.10
  123.7 2.2 convolution_bitcast_fusion.3
  126.7 1.2 fusion.9
  129.1 4.8 %all-to-all-start.3 = ((f32[8,128,2,128]{1,3,2,0:T(8,128)}), f32[8,128,2,128]{1,3,2,0:T(8,128)}, u32[]{:S(2)}, u32[]{:S(2)}) async-start(f32[8,128,2,128]{1,3,2,0:T(8,128)} %bitcast.192), calls=%async_computation.3 | async-start | bytes 2097152 | tf_op jit(solution)/shard_map/all_to_all | solution.py:63
  133.9 3.4 %convolution_bitcast_fusion.4 = f32[128,1,2,256]{0,3,2,1:T(8,128)} fusion(f32[1024,2,256]{0,2,1:T(8,128)} %copy-done.5, f32[1024,2,128]{2,0,1:T(8,128)S(1)} %bitcast.188), kind=kOutput, calls=%fused_computation.22 | convolution fusion | flops 402653184 | bytes 3407872 | tf_op jit(solution)/shard_map/tnd,tnf->dnf/dot_general | solution.py:126
  139.5 1.7 copy.143
  141.2 7.9 %all-to-all-done.3 = f32[8,128,2,128]{1,3,2,0:T(8,128)} async-done(((f32[8,128,2,128]{1,3,2,0:T(8,128)}), f32[8,128,2,128]{1,3,2,0:T(8,128)}, u32[]{:S(2)}, u32[]{:S(2)}) %all-to-all-start.3) | async-done | bytes 1048608 | tf_op jit(solution)/shard_map/all_to_all | solution.py:63
  149.1 5.1 %all-to-all-start.4 = ((f32[32,1,6144]{2,1,0:T(1,128)}), f32[32,1,6144]{2,1,0:T(1,128)}, u32[]{:S(2)}, u32[]{:S(2)}) async-start(f32[32,1,6144]{2,1,0:T(1,128)} %copy.143), calls=%async_computation.4 | async-start | bytes 1572864 | tf_op jit(solution)/shard_map/all_to_all | solution.py:63
  154.2 2.5 fusion.14
  156.7 3.1 %multiply_reduce_fusion.1 = (f32[2048]{0:T(1024)S(1)}, f32[2048]{0:T(1024)S(1)}, f32[128,2048]{0,1:T(8,128)S(1)}) fusion(f32[128,2048]{0,1:T(8,128)} %copy-done.4, f32[128,2048]{0,1:T(8,128)} %collective-permute-done.1, f32[128]{0:T(128)S(1)} %broadcast_multiply_fusion.2, f32[128,2048]{0,1:T(8,128)S(1)} %get-tuple-element.65, f32[2048]{0:T(1024)S(1)} %copy-done.18, ...), kind=kLoop, calls=%fused_computation.38 | loop fusion | flops 3141632 | bytes 6317056 | tf_op jit(solution)/shard_map/reduce_sum | solution.py:51
  160.8 13.7 %all-to-all-done.4 = f32[32,1,6144]{2,1,0:T(1,128)} async-done(((f32[32,1,6144]{2,1,0:T(1,128)}), f32[32,1,6144]{2,1,0:T(1,128)}, u32[]{:S(2)}, u32[]{:S(2)}) %all-to-all-start.4) | async-done | bytes 786464 | tf_op jit(solution)/shard_map/all_to_all | solution.py:63
  174.4 1.4 bitcast_reduce_fusion
  176.2 5.0 %collective-permute-start.4 = (f32[49152]{0:T(1024)S(1)}, f32[49152]{0:T(1024)S(1)}, u32[]{:S(2)}, u32[]{:S(2)}) collective-permute-start(f32[49152]{0:T(1024)S(1)} %pad_maximum_fusion.2), channel_id=1, source_target_pairs={{0,32},{32,0},{64,96},{96,64},{128,160},{160,128},{192,224},{224,1... | collective-permute-start | bytes 589832 | tf_op jit(solution)/shard_map/ppermute | solution.py:30
  183.0 2.9 %collective-permute-done.4 = f32[49152]{0:T(1024)S(1)} collective-permute-done((f32[49152]{0:T(1024)S(1)}, f32[49152]{0:T(1024)S(1)}, u32[]{:S(2)}, u32[]{:S(2)}) %collective-permute-start.4) | collective-permute-done | bytes 196640 | tf_op jit(solution)/shard_map/ppermute | solution.py:30
  185.9 1.3 collective-permute-start.5
  187.2 2.5 multiply_reduce_fusion.3
  191.9 1.3 fusion.11
  194.1 5.5 %all-to-all-start.5 = ((f32[32,1,1088]{2,1,0:T(1,128)}), f32[32,1,1088]{2,1,0:T(1,128)S(1)}, u32[]{:S(2)}, u32[]{:S(2)}) async-start(f32[32,1,1088]{2,1,0:T(1,128)} %all_to_all.41), calls=%async_computation.5 | async-start | bytes 294912 | tf_op jit(solution)/shard_map/all_to_all | solution.py:63
  200.6 2.8 %collective-permute-start.6 = (f32[49152]{0:T(1024)S(1)}, f32[49152]{0:T(1024)S(1)}, u32[]{:S(2)}, u32[]{:S(2)}) collective-permute-start(f32[49152]{0:T(1024)S(1)} %add.109), channel_id=1, source_target_pairs={{0,128},{128,0},{32,160},{160,32},{64,192},{192,64},{96,224},{224,... | collective-permute-start | bytes 589832 | tf_op jit(solution)/shard_map/ppermute | solution.py:30
  203.4 7.9 %all-to-all-done.5 = f32[32,1,1088]{2,1,0:T(1,128)S(1)} async-done(((f32[32,1,1088]{2,1,0:T(1,128)}), f32[32,1,1088]{2,1,0:T(1,128)S(1)}, u32[]{:S(2)}, u32[]{:S(2)}) %all-to-all-start.5) | async-done | bytes 139296 | tf_op jit(solution)/shard_map/all_to_all | solution.py:63
  212.3 1.7 collective-permute-done.7
  215.0 1.5 collective-permute-done.8
  216.5 2.5 collective-permute-start.9
  221.2 8.8 %all-to-all-start.6 = ((f32[32,1,1088]{2,1,0:T(1,128)}), f32[32,1,1088]{2,1,0:T(1,128)S(1)}, u32[]{:S(2)}, u32[]{:S(2)}) async-start(f32[32,1,1088]{2,1,0:T(1,128)} %broadcast_in_dim.8), calls=%async_computation.6 | async-start | bytes 294912 | tf_op jit(solution)/shard_map/all_to_all | solution.py:63
  230.7 38.3 %all-to-all-done.6 = f32[32,1,1088]{2,1,0:T(1,128)S(1)} async-done(((f32[32,1,1088]{2,1,0:T(1,128)}), f32[32,1,1088]{2,1,0:T(1,128)S(1)}, u32[]{:S(2)}, u32[]{:S(2)}) %all-to-all-start.6) | async-done | bytes 139296 | tf_op jit(solution)/shard_map/all_to_all | solution.py:63
  272.1 2.0 fusion.1
  274.0 1.3 copy.147
  (127 shorter events, 30.7 us)
Async XLA Ops:
  0.6 18.5 %copy-start = (f32[128,128]{1,0:T(8,128)S(1)}, f32[128,128]{1,0:T(8,128)}, u32[]{:S(2)}) copy-start(f32[128,128]{1,0:T(8,128)} %param.10) | copy-start | bytes 196612
  0.6 36.4 %collective-permute-start = (f32[1,128,2048]{2,1,0:T(8,128)}, f32[1,128,2048]{2,1,0:T(8,128)S(1)}, u32[]{:S(2)}, u32[]{:S(2)}) collective-permute-start(f32[1,128,2048]{2,1,0:T(8,128)} %param.8), channel_id=1, source_target_pairs={{0,16},{16,0},{1,17},{17,1},{2,18},{18,2},{3,19},{19,3},{4,20},{20... | collective-permute-start | bytes 3145736 | tf_op jit(solution)/shard_map/ppermute | solution.py:30
  10.0 1.0 copy-start.3
  11.0 6.9 %copy-start.22 = (f32[8,16,128]{2,1,0:T(8,128)S(1)}, f32[8,16,128]{2,1,0:T(8,128)}, u32[]{:S(2)}) copy-start(f32[8,16,128]{2,1,0:T(8,128)} %param.15) | copy-start | bytes 196612
  11.1 7.0 %copy-start.17 = (f32[4,2,16,256]{3,2,1,0:T(8,128)S(1)}, f32[4,2,16,256]{3,2,1,0:T(8,128)}, u32[]{:S(2)}) copy-start(f32[4,2,16,256]{3,2,1,0:T(8,128)} %param.14) | copy-start | bytes 393220
  12.4 6.7 %copy-start.1 = (f32[1,128,2048]{2,1,0:T(8,128)S(1)}, f32[1,128,2048]{2,1,0:T(8,128)}, u32[]{:S(2)}) copy-start(f32[1,128,2048]{2,1,0:T(8,128)} %param.8) | copy-start | bytes 3145732
  12.4 49.9 %all-to-all-start.1 = ((f32[8,128,2,128]{3,1,2,0:T(8,128)}), f32[8,128,2,128]{3,1,2,0:T(8,128)S(1)}, u32[]{:S(2)}, u32[]{:S(2)}) async-start(f32[8,128,2,128]{3,1,2,0:T(8,128)} %copy.131), calls=%async_computation.1 | async-start | bytes 2097152 | tf_op jit(solution)/shard_map/all_to_all | solution.py:63
  19.2 55.0 %copy-start.19 = (f32[1,1,2048]{2,1,0:T(1,128)}, f32[1,1,2048]{2,1,0:T(1,128)S(1)}, u32[]{:S(2)}) copy-start(f32[1,1,2048]{2,1,0:T(1,128)S(1)} %get-tuple-element.70) | copy-start | bytes 24580
  19.2 55.0 %copy-start.20 = (f32[1,1,2048]{2,1,0:T(1,128)}, f32[1,1,2048]{2,1,0:T(1,128)S(1)}, u32[]{:S(2)}) copy-start(f32[1,1,2048]{2,1,0:T(1,128)S(1)} %get-tuple-element.71) | copy-start | bytes 24580
  20.2 21.0 %copy-start.2 = (f32[128,2048]{0,1:T(8,128)}, f32[128,2048]{0,1:T(8,128)S(1)}, u32[]{:S(2)}) copy-start(f32[128,2048]{0,1:T(8,128)S(1)} %convolution_bitcast_fusion.2) | copy-start | bytes 3145732
  37.0 1.0 copy-start.11
  41.2 33.0 %copy-start.4 = (f32[128,2048]{0,1:T(8,128)}, f32[128,2048]{0,1:T(8,128)S(1)}, u32[]{:S(2)}) copy-start(f32[128,2048]{0,1:T(8,128)S(1)} %get-tuple-element.74) | copy-start | bytes 3145732
  41.2 33.0 %collective-permute-start.1 = (f32[128,2048]{0,1:T(8,128)S(1)}, f32[128,2048]{0,1:T(8,128)}, u32[]{:S(2)}, u32[]{:S(2)}) collective-permute-start(f32[128,2048]{0,1:T(8,128)S(1)} %get-tuple-element.74), channel_id=1, source_target_pairs={{0,1},{1,0},{2,3},{3,2},{4,5},{5,4},{6,7},{7,6},{8,9},{9,8},{10,11... | collective-permute-start | bytes 3145736 | tf_op jit(solution)/shard_map/ppermute | solution.py:30
  62.3 11.9 %copy-start.6 = (f32[8,128,2,128]{3,1,2,0:T(8,128)}, f32[8,128,2,128]{3,1,2,0:T(8,128)S(1)}, u32[]{:S(2)}) copy-start(f32[8,128,2,128]{3,1,2,0:T(8,128)S(1)} %all-to-all-done.1) | copy-start | bytes 3145732
  62.3 30.6 %all-to-all-start = ((f32[32,1,6144]{2,1,0:T(1,128)}), f32[32,1,6144]{2,1,0:T(1,128)}, u32[]{:S(2)}, u32[]{:S(2)}) async-start(f32[32,1,6144]{2,1,0:T(1,128)} %all_to_all.33), calls=%async_computation | async-start | bytes 1572864 | tf_op jit(solution)/shard_map/all_to_all | solution.py:63
  74.2 2.0 copy-start.18
  76.2 25.9 %copy-start.7 = (f32[8,128,2,128]{3,1,2,0:T(8,128)S(1)}, f32[8,128,2,128]{3,1,2,0:T(8,128)}, u32[]{:S(2)}) copy-start(f32[8,128,2,128]{3,1,2,0:T(8,128)} %copy-done.6) | copy-start | bytes 3145732
  92.9 23.8 %all-to-all-start.2 = ((f32[8,128,2,128]{1,3,2,0:T(8,128)}), f32[8,128,2,128]{1,3,2,0:T(8,128)}, u32[]{:S(2)}, u32[]{:S(2)}) async-start(f32[8,128,2,128]{1,3,2,0:T(8,128)} %bitcast.23), calls=%async_computation.2 | async-start | bytes 2097152 | tf_op jit(solution)/shard_map/all_to_all | solution.py:63
  105.5 7.9 %copy-start.9 = (f32[8,128,2,128]{3,1,0,2:T(8,128)S(1)}, f32[8,128,2,128]{3,1,0,2:T(8,128)}, u32[]{:S(2)}) copy-start(f32[8,128,2,128]{3,1,0,2:T(8,128)} %copy.132) | copy-start | bytes 3145732
  113.3 4.9 %copy-start.14 = (f32[128,1,2,256]{0,3,2,1:T(8,128)S(1)}, f32[128,1,2,256]{0,3,2,1:T(8,128)}, u32[]{:S(2)}) copy-start(f32[128,1,2,256]{0,3,2,1:T(8,128)} %copy.155) | copy-start | bytes 786436
  118.2 1.6 copy-start.13
  118.2 1.6 copy-start.15
  119.8 1.7 copy-start.10
  121.5 4.4 %copy-start.5 = (f32[1024,2,256]{0,2,1:T(8,128)}, f32[1024,2,256]{0,2,1:T(8,128)S(1)}, u32[]{:S(2)}) copy-start(f32[1024,2,256]{0,2,1:T(8,128)S(1)} %get-tuple-element.76) | copy-start | bytes 6291460
  129.1 20.0 %all-to-all-start.3 = ((f32[8,128,2,128]{1,3,2,0:T(8,128)}), f32[8,128,2,128]{1,3,2,0:T(8,128)}, u32[]{:S(2)}, u32[]{:S(2)}) async-start(f32[8,128,2,128]{1,3,2,0:T(8,128)} %bitcast.192), calls=%async_computation.3 | async-start | bytes 2097152 | tf_op jit(solution)/shard_map/all_to_all | solution.py:63
  133.9 3.4 %copy-start.16 = (f32[256,2,128]{2,0,1:T(8,128)S(1)}, f32[256,2,128]{2,0,1:T(8,128)}, u32[]{:S(2)}) copy-start(f32[256,2,128]{2,0,1:T(8,128)} %fusion.10) | copy-start | bytes 786436
  149.1 25.3 %all-to-all-start.4 = ((f32[32,1,6144]{2,1,0:T(1,128)}), f32[32,1,6144]{2,1,0:T(1,128)}, u32[]{:S(2)}, u32[]{:S(2)}) async-start(f32[32,1,6144]{2,1,0:T(1,128)} %copy.143), calls=%async_computation.4 | async-start | bytes 1572864 | tf_op jit(solution)/shard_map/all_to_all | solution.py:63
  156.7 3.7 %copy-start.21 = (f32[1,1,2048]{2,1,0:T(1,128)S(1)}, f32[1,1,2048]{2,1,0:T(1,128)}, u32[]{:S(2)}) copy-start(f32[1,1,2048]{2,1,0:T(1,128)} %copy-done.20) | copy-start | bytes 24580
  176.2 9.7 %collective-permute-start.4 = (f32[49152]{0:T(1024)S(1)}, f32[49152]{0:T(1024)S(1)}, u32[]{:S(2)}, u32[]{:S(2)}) collective-permute-start(f32[49152]{0:T(1024)S(1)} %pad_maximum_fusion.2), channel_id=1, source_target_pairs={{0,32},{32,0},{64,96},{96,64},{128,160},{160,128},{192,224},{224,1... | collective-permute-start | bytes 589832 | tf_op jit(solution)/shard_map/ppermute | solution.py:30
  182.0 5.2 %collective-permute-start.2 = (f32[128,2048]{0,1:T(8,128)S(1)}, f32[128,2048]{0,1:T(8,128)S(1)}, u32[]{:S(2)}, u32[]{:S(2)}) collective-permute-start(f32[128,2048]{0,1:T(8,128)S(1)} %broadcast_multiply_fusion), channel_id=1, source_target_pairs={{0,1},{1,0},{2,3},{3,2},{4,5},{5,4},{6,7},{7,6},{8,9},{9,8},{10,11... | collective-permute-start | bytes 3145736 | tf_op jit(solution)/shard_map/ppermute | solution.py:30
  185.9 13.7 %collective-permute-start.5 = (f32[49152]{0:T(1024)S(1)}, f32[49152]{0:T(1024)}, u32[]{:S(2)}, u32[]{:S(2)}) collective-permute-start(f32[49152]{0:T(1024)S(1)} %fusion.33), channel_id=1, source_target_pairs={{0,64},{64,0},{32,96},{96,32},{128,192},{192,128},{160,224},{224,1... | collective-permute-start | bytes 589832 | tf_op jit(solution)/shard_map/ppermute | solution.py:30
  187.2 2.5 copy-start.24
  189.7 1.2 copy-start.12
  190.9 2.3 copy-start.8
  190.9 2.3 copy-start.23
  194.1 17.2 %all-to-all-start.5 = ((f32[32,1,1088]{2,1,0:T(1,128)}), f32[32,1,1088]{2,1,0:T(1,128)S(1)}, u32[]{:S(2)}, u32[]{:S(2)}) async-start(f32[32,1,1088]{2,1,0:T(1,128)} %all_to_all.41), calls=%async_computation.5 | async-start | bytes 294912 | tf_op jit(solution)/shard_map/all_to_all | solution.py:63
  200.6 14.3 %collective-permute-start.6 = (f32[49152]{0:T(1024)S(1)}, f32[49152]{0:T(1024)S(1)}, u32[]{:S(2)}, u32[]{:S(2)}) collective-permute-start(f32[49152]{0:T(1024)S(1)} %add.109), channel_id=1, source_target_pairs={{0,128},{128,0},{32,160},{160,32},{64,192},{192,64},{96,224},{224,... | collective-permute-start | bytes 589832 | tf_op jit(solution)/shard_map/ppermute | solution.py:30
  211.4 2.6 collective-permute-start.7
  214.0 2.5 collective-permute-start.8
  214.3 57.8 %collective-permute-start.3 = (f32[128,2048]{0,1:T(8,128)}, f32[128,2048]{0,1:T(8,128)}, u32[]{:S(2)}, u32[]{:S(2)}) collective-permute-start(f32[128,2048]{0,1:T(8,128)} %copy-done.8), channel_id=1, source_target_pairs={{0,16},{16,0},{1,17},{17,1},{2,18},{18,2},{3,19},{19,3},{4,20},{20... | collective-permute-start | bytes 3145736 | tf_op jit(solution)/shard_map/ppermute | solution.py:30
  216.5 4.0 %collective-permute-start.9 = (f32[1088]{0:T(1024)S(1)}, f32[1088]{0:T(1024)S(1)}, u32[]{:S(2)}, u32[]{:S(2)}) collective-permute-start(f32[1088]{0:T(1024)S(1)} %add.113), channel_id=1, source_target_pairs={{0,128},{128,0},{32,160},{160,32},{64,192},{192,64},{96,224},{224,... | collective-permute-start | bytes 13064 | tf_op jit(solution)/shard_map/ppermute | solution.py:30
  221.2 47.7 %all-to-all-start.6 = ((f32[32,1,1088]{2,1,0:T(1,128)}), f32[32,1,1088]{2,1,0:T(1,128)S(1)}, u32[]{:S(2)}, u32[]{:S(2)}) async-start(f32[32,1,1088]{2,1,0:T(1,128)} %broadcast_in_dim.8), calls=%async_computation.6 | async-start | bytes 294912 | tf_op jit(solution)/shard_map/all_to_all | solution.py:63
where the time goes:
time: 277 us; the launch traced here: 275 us
  waiting for transfers between devices  107 us (39%)
  starting transfers between devices  87.8 us (32%)
  local copies, waits for them, and re-layouts  34.8 us (13%)
  matrix products  24.2 us (9%)
  other arithmetic  20.4 us (7%)
    all_to_all x7, waiting for transfers between devices, exchange(): return lax.all_to_all(x, axis, 0, 0, tiled=True)  83 us
    all_to_all x7, starting transfers between devices, exchange(): return lax.all_to_all(x, axis, 0, 0, tiled=True)  48.5 us
    ppermute x10, starting transfers between devices, from_partner(): return lax.ppermute(block, axis, route)  39.3 us
    ppermute x10, waiting for transfers between devices, from_partner(): return lax.ppermute(block, axis, route)  23.8 us
    unnamed x59, local copies, waits for them, and re-layouts  11.7 us
    all_to_all x5, local copies, waits for them, and re-layouts, exchange(): return lax.all_to_all(x, axis, 0, 0, tiled=True)  8.21 us
    reduce_sum x2, other arithmetic, backward_section(): jnp.sum(grad * field, axis=0)  5.55 us
  transfers between devices with their start and end apart: 17, of which 10 were waited for; matrix products, arithmetic and copies ran while one was open for 20% of the time, Pallas kernels for 0%

commit v1 on v0

--- a/solution.py
+++ b/solution.py
@@ -54,7 +54,7 @@
 
 
 def psum_doubling(x, axis):
-    for bit in range(axis_count(axis).bit_length() - 1):
+    for bit in reversed(range(axis_count(axis).bit_length() - 1)):
         x = x + from_partner(x, axis, bit)
     return x
 

time: 277 us -> 293 us (1.058)
  waiting for transfers between devices: 107 us -> 123 us
    ppermute x10, waiting for transfers between devices: 23.8 us -> 66.7 us  [from_partner(): return lax.ppermute(block, axis, route)]
    all_to_all x7, waiting for transfers between devices: 83 us -> 56.6 us  [exchange(): return lax.all_to_all(x, axis, 0, 0, tiled=True)]
  transfers between devices with their start and end apart: 17 -> 17, of which waited for: 10 -> 10; matrix products, arithmetic and copies ran while one was open for 20% -> 19% of each run, Pallas kernels for 0% -> 0%
where the time goes in v1:
time: 293 us; the launch traced here: 291 us
  waiting for transfers between devices  123 us (42%)
  starting transfers between devices  87.3 us (30%)
  local copies, waits for them, and re-layouts  34.8 us (12%)
  matrix products  24.2 us (8%)
  other arithmetic  20.4 us (7%)
    ppermute x10, waiting for transfers between devices, from_partner(): return lax.ppermute(block, axis, route)  66.7 us
    all_to_all x7, waiting for transfers between devices, exchange(): return lax.all_to_all(x, axis, 0, 0, tiled=True)  56.6 us
    all_to_all x7, starting transfers between devices, exchange(): return lax.all_to_all(x, axis, 0, 0, tiled=True)  50.9 us
    ppermute x10, starting transfers between devices, from_partner(): return lax.ppermute(block, axis, route)  36.5 us
    unnamed x59, local copies, waits for them, and re-layouts  11.7 us
    all_to_all x5, local copies, waits for them, and re-layouts, exchange(): return lax.all_to_all(x, axis, 0, 0, tiled=True)  8.21 us
  transfers between devices with their start and end apart: 17, of which 10 were waited for; matrix products, arithmetic and copies ran while one was open for 19% of the time, Pallas kernels for 0%

profile of v1, /device:TPU:1, one launch (start us, length us, event | category | flops | bytes accessed | tf_op | source)
XLA Modules:
  0.0 291.3 jit_solution(9972097837367241240)
XLA Ops:
  0.6 7.8 %collective-permute-start = (f32[1,128,2048]{2,1,0:T(8,128)}, f32[1,128,2048]{2,1,0:T(8,128)S(1)}, u32[]{:S(2)}, u32[]{:S(2)}) collective-permute-start(f32[1,128,2048]{2,1,0:T(8,128)} %param.8), channel_id=1, source_target_pairs={{0,16},{16,0},{1,17},{17,1},{2,18},{18,2},{3,19},{19,3},{4,20},{20... | collective-permute-start | bytes 3145736 | tf_op jit(solution)/shard_map/ppermute | solution.py:30
  8.5 1.5 copy.125
  11.1 1.3 copy.131
  12.4 5.6 %all-to-all-start.1 = ((f32[8,128,2,128]{3,1,2,0:T(8,128)}), f32[8,128,2,128]{3,1,2,0:T(8,128)S(1)}, u32[]{:S(2)}, u32[]{:S(2)}) async-start(f32[8,128,2,128]{3,1,2,0:T(8,128)} %copy.131), calls=%async_computation.1 | async-start | bytes 2097152 | tf_op jit(solution)/shard_map/all_to_all | solution.py:63
  20.2 16.8 %collective-permute-done = f32[1,128,2048]{2,1,0:T(8,128)S(1)} collective-permute-done((f32[1,128,2048]{2,1,0:T(8,128)}, f32[1,128,2048]{2,1,0:T(8,128)S(1)}, u32[]{:S(2)}, u32[]{:S(2)}) %collective-permute-start) | collective-permute-done | bytes 1048608 | tf_op jit(solution)/shard_map/ppermute | solution.py:30
  38.0 3.2 %multiply_add_fusion.1 = (f32[128,2048]{0,1:T(8,128)S(1)}, f32[128,2048]{0,1:T(8,128)}) fusion(f32[128,2048]{0,1:T(8,128)S(1)} %convolution_bitcast_fusion.2, f32[2048]{0:T(1024)S(1)} %bitcast.209, f32[2048]{0:T(1024)S(1)} %bitcast.204, f32[128,128]{1,0:T(8,128)S(1)} %copy-done, f32[1,128,2048]{2,1,0:T(8,128)} %copy-done.11), kind=kOutput, calls=%fused_computation.45 | convolution fusion | flops 202113024 | bytes 4276224 | tf_op jit(solution)/shard_map/ij,kjd->kid/dot_general | solution.py:103
  41.2 17.1 %collective-permute-start.1 = (f32[128,2048]{0,1:T(8,128)S(1)}, f32[128,2048]{0,1:T(8,128)}, u32[]{:S(2)}, u32[]{:S(2)}) collective-permute-start(f32[128,2048]{0,1:T(8,128)S(1)} %get-tuple-element.74), channel_id=1, source_target_pairs={{0,1},{1,0},{2,3},{3,2},{4,5},{5,4},{6,7},{7,6},{8,9},{9,8},{10,11... | collective-permute-start | bytes 3145736 | tf_op jit(solution)/shard_map/ppermute | solution.py:30
  59.3 3.0 %all_to_all.33 = f32[32,1,6144]{2,1,0:T(1,128)} reshape(f32[4,8,6144]{2,1,0:T(8,128)} %broadcast_in_dim.6) | data formatting | bytes 1572864 | tf_op jit(solution)/shard_map/all_to_all | solution.py:63
  62.3 10.6 %all-to-all-start = ((f32[32,1,6144]{2,1,0:T(1,128)}), f32[32,1,6144]{2,1,0:T(1,128)}, u32[]{:S(2)}, u32[]{:S(2)}) async-start(f32[32,1,6144]{2,1,0:T(1,128)} %all_to_all.33), calls=%async_computation | async-start | bytes 1572864 | tf_op jit(solution)/shard_map/all_to_all | solution.py:63
  72.8 1.3 copy.126
  74.2 1.9 multiply_reduce_fusion.5
  76.2 1.4 multiply_multiply_fusion
  77.6 15.3 %all-to-all-done = f32[32,1,6144]{2,1,0:T(1,128)} async-done(((f32[32,1,6144]{2,1,0:T(1,128)}), f32[32,1,6144]{2,1,0:T(1,128)}, u32[]{:S(2)}, u32[]{:S(2)}) %all-to-all-start) | async-done | bytes 786464 | tf_op jit(solution)/shard_map/all_to_all | solution.py:63
  92.9 8.1 %all-to-all-start.2 = ((f32[8,128,2,128]{1,3,2,0:T(8,128)}), f32[8,128,2,128]{1,3,2,0:T(8,128)}, u32[]{:S(2)}, u32[]{:S(2)}) async-start(f32[8,128,2,128]{1,3,2,0:T(8,128)} %bitcast.23), calls=%async_computation.2 | async-start | bytes 2097152 | tf_op jit(solution)/shard_map/all_to_all | solution.py:63
  103.2 1.4 copy.169
  105.5 2.4 reshape.193
  108.8 1.9 fusion.35
  110.7 1.8 copy.155
  113.3 3.3 %fusion.31 = f32[2,256,1024]{2,1,0:T(8,128)} fusion(f32[1024,2,128]{2,0,1:T(8,128)S(1)} %bitcast.190, f32[256,2,128]{2,1,0:T(2,128)} %reshape.194), kind=kOutput, calls=%fused_computation.64 | convolution fusion | flops 402653184 | bytes 3407872 | tf_op jit(solution)/shard_map/tnd,fnd->tnf/dot_general | solution.py:118
  116.7 1.6 copy.135
  119.8 1.7 fusion.6
  121.6 2.2 fusion.10
  123.7 2.2 convolution_bitcast_fusion.3
  129.1 4.8 %all-to-all-start.3 = ((f32[8,128,2,128]{1,3,2,0:T(8,128)}), f32[8,128,2,128]{1,3,2,0:T(8,128)}, u32[]{:S(2)}, u32[]{:S(2)}) async-start(f32[8,128,2,128]{1,3,2,0:T(8,128)} %bitcast.192), calls=%async_computation.3 | async-start | bytes 2097152 | tf_op jit(solution)/shard_map/all_to_all | solution.py:63
  133.9 3.4 %convolution_bitcast_fusion.4 = f32[128,1,2,256]{0,3,2,1:T(8,128)} fusion(f32[1024,2,256]{0,2,1:T(8,128)} %copy-done.5, f32[1024,2,128]{2,0,1:T(8,128)S(1)} %bitcast.188), kind=kOutput, calls=%fused_computation.22 | convolution fusion | flops 402653184 | bytes 3407872 | tf_op jit(solution)/shard_map/tnd,tnf->dnf/dot_general | solution.py:126
  139.5 1.7 copy.143
  141.2 7.9 %all-to-all-done.3 = f32[8,128,2,128]{1,3,2,0:T(8,128)} async-done(((f32[8,128,2,128]{1,3,2,0:T(8,128)}), f32[8,128,2,128]{1,3,2,0:T(8,128)}, u32[]{:S(2)}, u32[]{:S(2)}) %all-to-all-start.3) | async-done | bytes 1048608 | tf_op jit(solution)/shard_map/all_to_all | solution.py:63
  149.1 5.1 %all-to-all-start.4 = ((f32[32,1,6144]{2,1,0:T(1,128)}), f32[32,1,6144]{2,1,0:T(1,128)}, u32[]{:S(2)}, u32[]{:S(2)}) async-start(f32[32,1,6144]{2,1,0:T(1,128)} %copy.143), calls=%async_computation.4 | async-start | bytes 1572864 | tf_op jit(solution)/shard_map/all_to_all | solution.py:63
  154.2 2.5 fusion.14
  156.7 3.1 %multiply_reduce_fusion.1 = (f32[2048]{0:T(1024)S(1)}, f32[2048]{0:T(1024)S(1)}, f32[128,2048]{0,1:T(8,128)S(1)}) fusion(f32[128,2048]{0,1:T(8,128)} %copy-done.4, f32[128,2048]{0,1:T(8,128)} %collective-permute-done.1, f32[128]{0:T(128)S(1)} %broadcast_multiply_fusion.2, f32[128,2048]{0,1:T(8,128)S(1)} %get-tuple-element.65, f32[2048]{0:T(1024)S(1)} %copy-done.18, ...), kind=kLoop, calls=%fused_computation.38 | loop fusion | flops 3141632 | bytes 6317056 | tf_op jit(solution)/shard_map/reduce_sum | solution.py:51
  160.8 13.7 %all-to-all-done.4 = f32[32,1,6144]{2,1,0:T(1,128)} async-done(((f32[32,1,6144]{2,1,0:T(1,128)}), f32[32,1,6144]{2,1,0:T(1,128)}, u32[]{:S(2)}, u32[]{:S(2)}) %all-to-all-start.4) | async-done | bytes 786464 | tf_op jit(solution)/shard_map/all_to_all | solution.py:63
  174.4 1.4 bitcast_reduce_fusion
  176.2 2.8 collective-permute-start.4
  179.8 4.2 %collective-permute-start.2 = (f32[128,2048]{0,1:T(8,128)S(1)}, f32[128,2048]{0,1:T(8,128)S(1)}, u32[]{:S(2)}, u32[]{:S(2)}) collective-permute-start(f32[128,2048]{0,1:T(8,128)S(1)} %broadcast_multiply_fusion), channel_id=1, source_target_pairs={{0,1},{1,0},{2,3},{3,2},{4,5},{5,4},{6,7},{7,6},{8,9},{9,8},{10,11... | collective-permute-start | bytes 3145736 | tf_op jit(solution)/shard_map/ppermute | solution.py:30
  184.5 1.8 collective-permute-done.2
  186.3 2.5 multiply_reduce_fusion.3
  191.0 1.3 fusion.11
  193.2 8.0 %all-to-all-start.5 = ((f32[32,1,1088]{2,1,0:T(1,128)}), f32[32,1,1088]{2,1,0:T(1,128)S(1)}, u32[]{:S(2)}, u32[]{:S(2)}) async-start(f32[32,1,1088]{2,1,0:T(1,128)} %all_to_all.41), calls=%async_computation.5 | async-start | bytes 294912 | tf_op jit(solution)/shard_map/all_to_all | solution.py:63
  202.2 1.7 collective-permute-start.6
  203.9 9.2 %all-to-all-done.5 = f32[32,1,1088]{2,1,0:T(1,128)S(1)} async-done(((f32[32,1,1088]{2,1,0:T(1,128)}), f32[32,1,1088]{2,1,0:T(1,128)S(1)}, u32[]{:S(2)}, u32[]{:S(2)}) %all-to-all-start.5) | async-done | bytes 139296 | tf_op jit(solution)/shard_map/all_to_all | solution.py:63
  213.2 1.4 collective-permute-start.7
  214.6 2.7 collective-permute-done.7
  217.6 2.2 collective-permute-done.8
  221.1 43.1 %collective-permute-done.9 = f32[1088]{0:T(1024)S(1)} collective-permute-done((f32[1088]{0:T(1024)S(1)}, f32[1088]{0:T(1024)S(1)}, u32[]{:S(2)}, u32[]{:S(2)}) %collective-permute-start.9) | collective-permute-done | bytes 4384 | tf_op jit(solution)/shard_map/ppermute | solution.py:30
  265.0 8.7 %all-to-all-start.6 = ((f32[32,1,1088]{2,1,0:T(1,128)}), f32[32,1,1088]{2,1,0:T(1,128)S(1)}, u32[]{:S(2)}, u32[]{:S(2)}) async-start(f32[32,1,1088]{2,1,0:T(1,128)} %broadcast_in_dim.8), calls=%async_computation.6 | async-start | bytes 294912 | tf_op jit(solution)/shard_map/all_to_all | solution.py:63
  274.3 10.6 %all-to-all-done.6 = f32[32,1,1088]{2,1,0:T(1,128)S(1)} async-done(((f32[32,1,1088]{2,1,0:T(1,128)}), f32[32,1,1088]{2,1,0:T(1,128)S(1)}, u32[]{:S(2)}, u32[]{:S(2)}) %all-to-all-start.6) | async-done | bytes 139296 | tf_op jit(solution)/shard_map/all_to_all | solution.py:63
  288.0 2.0 fusion.1
  290.0 1.3 copy.147
  (127 shorter events, 29.6 us)
Async XLA Ops:
  0.6 18.5 %copy-start = (f32[128,128]{1,0:T(8,128)S(1)}, f32[128,128]{1,0:T(8,128)}, u32[]{:S(2)}) copy-start(f32[128,128]{1,0:T(8,128)} %param.10) | copy-start | bytes 196612
  0.6 36.4 %collective-permute-start = (f32[1,128,2048]{2,1,0:T(8,128)}, f32[1,128,2048]{2,1,0:T(8,128)S(1)}, u32[]{:S(2)}, u32[]{:S(2)}) collective-permute-start(f32[1,128,2048]{2,1,0:T(8,128)} %param.8), channel_id=1, source_target_pairs={{0,16},{16,0},{1,17},{17,1},{2,18},{18,2},{3,19},{19,3},{4,20},{20... | collective-permute-start | bytes 3145736 | tf_op jit(solution)/shard_map/ppermute | solution.py:30
  10.0 1.0 copy-start.3
  11.0 6.9 %copy-start.22 = (f32[8,16,128]{2,1,0:T(8,128)S(1)}, f32[8,16,128]{2,1,0:T(8,128)}, u32[]{:S(2)}) copy-start(f32[8,16,128]{2,1,0:T(8,128)} %param.15) | copy-start | bytes 196612
  11.1 7.0 %copy-start.17 = (f32[4,2,16,256]{3,2,1,0:T(8,128)S(1)}, f32[4,2,16,256]{3,2,1,0:T(8,128)}, u32[]{:S(2)}) copy-start(f32[4,2,16,256]{3,2,1,0:T(8,128)} %param.14) | copy-start | bytes 393220
  12.4 6.7 %copy-start.1 = (f32[1,128,2048]{2,1,0:T(8,128)S(1)}, f32[1,128,2048]{2,1,0:T(8,128)}, u32[]{:S(2)}) copy-start(f32[1,128,2048]{2,1,0:T(8,128)} %param.8) | copy-start | bytes 3145732
  12.4 49.9 %all-to-all-start.1 = ((f32[8,128,2,128]{3,1,2,0:T(8,128)}), f32[8,128,2,128]{3,1,2,0:T(8,128)S(1)}, u32[]{:S(2)}, u32[]{:S(2)}) async-start(f32[8,128,2,128]{3,1,2,0:T(8,128)} %copy.131), calls=%async_computation.1 | async-start | bytes 2097152 | tf_op jit(solution)/shard_map/all_to_all | solution.py:63
  19.2 55.0 %copy-start.19 = (f32[1,1,2048]{2,1,0:T(1,128)}, f32[1,1,2048]{2,1,0:T(1,128)S(1)}, u32[]{:S(2)}) copy-start(f32[1,1,2048]{2,1,0:T(1,128)S(1)} %get-tuple-element.70) | copy-start | bytes 24580
  19.2 55.0 %copy-start.20 = (f32[1,1,2048]{2,1,0:T(1,128)}, f32[1,1,2048]{2,1,0:T(1,128)S(1)}, u32[]{:S(2)}) copy-start(f32[1,1,2048]{2,1,0:T(1,128)S(1)} %get-tuple-element.71) | copy-start | bytes 24580
  20.2 21.0 %copy-start.2 = (f32[128,2048]{0,1:T(8,128)}, f32[128,2048]{0,1:T(8,128)S(1)}, u32[]{:S(2)}) copy-start(f32[128,2048]{0,1:T(8,128)S(1)} %convolution_bitcast_fusion.2) | copy-start | bytes 3145732
  37.0 1.0 copy-start.11
  41.2 33.0 %copy-start.4 = (f32[128,2048]{0,1:T(8,128)}, f32[128,2048]{0,1:T(8,128)S(1)}, u32[]{:S(2)}) copy-start(f32[128,2048]{0,1:T(8,128)S(1)} %get-tuple-element.74) | copy-start | bytes 3145732
  41.2 33.0 %collective-permute-start.1 = (f32[128,2048]{0,1:T(8,128)S(1)}, f32[128,2048]{0,1:T(8,128)}, u32[]{:S(2)}, u32[]{:S(2)}) collective-permute-start(f32[128,2048]{0,1:T(8,128)S(1)} %get-tuple-element.74), channel_id=1, source_target_pairs={{0,1},{1,0},{2,3},{3,2},{4,5},{5,4},{6,7},{7,6},{8,9},{9,8},{10,11... | collective-permute-start | bytes 3145736 | tf_op jit(solution)/shard_map/ppermute | solution.py:30
  62.3 11.9 %copy-start.6 = (f32[8,128,2,128]{3,1,2,0:T(8,128)}, f32[8,128,2,128]{3,1,2,0:T(8,128)S(1)}, u32[]{:S(2)}) copy-start(f32[8,128,2,128]{3,1,2,0:T(8,128)S(1)} %all-to-all-done.1) | copy-start | bytes 3145732
  62.3 30.6 %all-to-all-start = ((f32[32,1,6144]{2,1,0:T(1,128)}), f32[32,1,6144]{2,1,0:T(1,128)}, u32[]{:S(2)}, u32[]{:S(2)}) async-start(f32[32,1,6144]{2,1,0:T(1,128)} %all_to_all.33), calls=%async_computation | async-start | bytes 1572864 | tf_op jit(solution)/shard_map/all_to_all | solution.py:63
  74.2 2.0 copy-start.18
  76.2 25.9 %copy-start.7 = (f32[8,128,2,128]{3,1,2,0:T(8,128)S(1)}, f32[8,128,2,128]{3,1,2,0:T(8,128)}, u32[]{:S(2)}) copy-start(f32[8,128,2,128]{3,1,2,0:T(8,128)} %copy-done.6) | copy-start | bytes 3145732
  92.9 23.8 %all-to-all-start.2 = ((f32[8,128,2,128]{1,3,2,0:T(8,128)}), f32[8,128,2,128]{1,3,2,0:T(8,128)}, u32[]{:S(2)}, u32[]{:S(2)}) async-start(f32[8,128,2,128]{1,3,2,0:T(8,128)} %bitcast.23), calls=%async_computation.2 | async-start | bytes 2097152 | tf_op jit(solution)/shard_map/all_to_all | solution.py:63
  105.5 7.9 %copy-start.9 = (f32[8,128,2,128]{3,1,0,2:T(8,128)S(1)}, f32[8,128,2,128]{3,1,0,2:T(8,128)}, u32[]{:S(2)}) copy-start(f32[8,128,2,128]{3,1,0,2:T(8,128)} %copy.132) | copy-start | bytes 3145732
  113.3 4.9 %copy-start.14 = (f32[128,1,2,256]{0,3,2,1:T(8,128)S(1)}, f32[128,1,2,256]{0,3,2,1:T(8,128)}, u32[]{:S(2)}) copy-start(f32[128,1,2,256]{0,3,2,1:T(8,128)} %copy.155) | copy-start | bytes 786436
  118.2 1.6 copy-start.13
  118.2 1.6 copy-start.15
  119.8 1.7 copy-start.10
  121.5 4.4 %copy-start.5 = (f32[1024,2,256]{0,2,1:T(8,128)}, f32[1024,2,256]{0,2,1:T(8,128)S(1)}, u32[]{:S(2)}) copy-start(f32[1024,2,256]{0,2,1:T(8,128)S(1)} %get-tuple-element.76) | copy-start | bytes 6291460
  129.1 20.0 %all-to-all-start.3 = ((f32[8,128,2,128]{1,3,2,0:T(8,128)}), f32[8,128,2,128]{1,3,2,0:T(8,128)}, u32[]{:S(2)}, u32[]{:S(2)}) async-start(f32[8,128,2,128]{1,3,2,0:T(8,128)} %bitcast.192), calls=%async_computation.3 | async-start | bytes 2097152 | tf_op jit(solution)/shard_map/all_to_all | solution.py:63
  133.9 3.4 %copy-start.16 = (f32[256,2,128]{2,0,1:T(8,128)S(1)}, f32[256,2,128]{2,0,1:T(8,128)}, u32[]{:S(2)}) copy-start(f32[256,2,128]{2,0,1:T(8,128)} %fusion.10) | copy-start | bytes 786436
  149.1 25.3 %all-to-all-start.4 = ((f32[32,1,6144]{2,1,0:T(1,128)}), f32[32,1,6144]{2,1,0:T(1,128)}, u32[]{:S(2)}, u32[]{:S(2)}) async-start(f32[32,1,6144]{2,1,0:T(1,128)} %copy.143), calls=%async_computation.4 | async-start | bytes 1572864 | tf_op jit(solution)/shard_map/all_to_all | solution.py:63
  156.7 3.7 %copy-start.21 = (f32[1,1,2048]{2,1,0:T(1,128)S(1)}, f32[1,1,2048]{2,1,0:T(1,128)}, u32[]{:S(2)}) copy-start(f32[1,1,2048]{2,1,0:T(1,128)} %copy-done.20) | copy-start | bytes 24580
  176.2 7.9 %collective-permute-start.4 = (f32[49152]{0:T(1024)S(1)}, f32[49152]{0:T(1024)S(1)}, u32[]{:S(2)}, u32[]{:S(2)}) collective-permute-start(f32[49152]{0:T(1024)S(1)} %pad_maximum_fusion.2), channel_id=1, source_target_pairs={{0,128},{128,0},{32,160},{160,32},{64,192},{192,64},{96,224},{224,... | collective-permute-start | bytes 589832 | tf_op jit(solution)/shard_map/ppermute | solution.py:30
  179.8 6.5 %collective-permute-start.2 = (f32[128,2048]{0,1:T(8,128)S(1)}, f32[128,2048]{0,1:T(8,128)S(1)}, u32[]{:S(2)}, u32[]{:S(2)}) collective-permute-start(f32[128,2048]{0,1:T(8,128)S(1)} %broadcast_multiply_fusion), channel_id=1, source_target_pairs={{0,1},{1,0},{2,3},{3,2},{4,5},{5,4},{6,7},{7,6},{8,9},{9,8},{10,11... | collective-permute-start | bytes 3145736 | tf_op jit(solution)/shard_map/ppermute | solution.py:30
  184.1 17.1 %collective-permute-start.5 = (f32[49152]{0:T(1024)S(1)}, f32[49152]{0:T(1024)}, u32[]{:S(2)}, u32[]{:S(2)}) collective-permute-start(f32[49152]{0:T(1024)S(1)} %fusion.33), channel_id=1, source_target_pairs={{0,64},{64,0},{32,96},{96,32},{128,192},{192,128},{160,224},{224,1... | collective-permute-start | bytes 589832 | tf_op jit(solution)/shard_map/ppermute | solution.py:30
  186.3 2.5 copy-start.24
  188.8 1.2 copy-start.12
  190.0 2.3 copy-start.8
  190.0 2.3 copy-start.23
  193.2 19.8 %all-to-all-start.5 = ((f32[32,1,1088]{2,1,0:T(1,128)}), f32[32,1,1088]{2,1,0:T(1,128)S(1)}, u32[]{:S(2)}, u32[]{:S(2)}) async-start(f32[32,1,1088]{2,1,0:T(1,128)} %all_to_all.41), calls=%async_computation.5 | async-start | bytes 294912 | tf_op jit(solution)/shard_map/all_to_all | solution.py:63
  202.2 15.4 %collective-permute-start.6 = (f32[49152]{0:T(1024)S(1)}, f32[49152]{0:T(1024)S(1)}, u32[]{:S(2)}, u32[]{:S(2)}) collective-permute-start(f32[49152]{0:T(1024)S(1)} %add.109), channel_id=1, source_target_pairs={{0,32},{32,0},{64,96},{96,64},{128,160},{160,128},{192,224},{224,1... | collective-permute-start | bytes 589832 | tf_op jit(solution)/shard_map/ppermute | solution.py:30
  213.2 4.1 %collective-permute-start.7 = (f32[1088]{0:T(1024)S(1)}, f32[1088]{0:T(1024)S(1)}, u32[]{:S(2)}, u32[]{:S(2)}) collective-permute-start(f32[1088]{0:T(1024)S(1)} %reduce_sum.89), channel_id=1, source_target_pairs={{0,128},{128,0},{32,160},{160,32},{64,192},{192,64},{96,224},{224,... | collective-permute-start | bytes 13064 | tf_op jit(solution)/shard_map/ppermute | solution.py:30
  217.3 2.5 collective-permute-start.8
  217.3 70.7 %collective-permute-start.3 = (f32[128,2048]{0,1:T(8,128)}, f32[128,2048]{0,1:T(8,128)}, u32[]{:S(2)}, u32[]{:S(2)}) collective-permute-start(f32[128,2048]{0,1:T(8,128)} %copy-done.8), channel_id=1, source_target_pairs={{0,16},{16,0},{1,17},{17,1},{2,18},{18,2},{3,19},{19,3},{4,20},{20... | collective-permute-start | bytes 3145736 | tf_op jit(solution)/shard_map/ppermute | solution.py:30
  219.8 44.5 %collective-permute-start.9 = (f32[1088]{0:T(1024)S(1)}, f32[1088]{0:T(1024)S(1)}, u32[]{:S(2)}, u32[]{:S(2)}) collective-permute-start(f32[1088]{0:T(1024)S(1)} %add.113), channel_id=1, source_target_pairs={{0,32},{32,0},{64,96},{96,64},{128,160},{160,128},{192,224},{224,1... | collective-permute-start | bytes 13064 | tf_op jit(solution)/shard_map/ppermute | solution.py:30
  265.0 20.0 %all-to-all-start.6 = ((f32[32,1,1088]{2,1,0:T(1,128)}), f32[32,1,1088]{2,1,0:T(1,128)S(1)}, u32[]{:S(2)}, u32[]{:S(2)}) async-start(f32[32,1,1088]{2,1,0:T(1,128)} %broadcast_in_dim.8), calls=%async_computation.6 | async-start | bytes 294912 | tf_op jit(solution)/shard_map/all_to_all | solution.py:63

commit v2 on v0

--- a/solution.py
+++ b/solution.py
@@ -110,22 +110,19 @@
     normed = unit * gain
     x_blk = to_group(normed)
 
-    gate_val = jnp.einsum("tnd,dnf->tnf", x_blk, w_gu[:, 0], precision=HIGH)
-    up_val = jnp.einsum("tnd,dnf->tnf", x_blk, w_gu[:, 1], precision=HIGH)
+    both_val = jnp.einsum("tnd,dgnf->gtnf", x_blk, w_gu, precision=HIGH)
+    gate_val, up_val = both_val[0], both_val[1]
     sig = jax.nn.sigmoid(gate_val)
     act = gate_val * sig
     hidden = act * up_val
     grad_hidden = jnp.einsum("tnd,fnd->tnf", cot_blk, w_dn, precision=HIGH)
     grad_gate = grad_hidden * up_val * sig * (1.0 + gate_val * (1.0 - sig))
     grad_up = grad_hidden * act
-    grad_x = jnp.einsum("tnf,dnf->tnd", grad_gate, w_gu[:, 0], precision=HIGH) + jnp.einsum(
-        "tnf,dnf->tnd", grad_up, w_gu[:, 1], precision=HIGH
-    )
+    grad_both = jnp.stack([grad_gate, grad_up])
+    grad_x = jnp.einsum("gtnf,dgnf->tnd", grad_both, w_gu, precision=HIGH)
     grad_normed = from_group(grad_x)
 
-    d_gate = jnp.einsum("tnd,tnf->dnf", x_blk, grad_gate, precision=HIGH)
-    d_up = jnp.einsum("tnd,tnf->dnf", x_blk, grad_up, precision=HIGH)
-    d_gu = jnp.stack([d_gate, d_up], axis=1).reshape(count, -1)
+    d_gu = jnp.einsum("tnd,gtnf->dgnf", x_blk, grad_both, precision=HIGH).reshape(count, -1)
     d_dn = jnp.einsum("tnf,tnd->fnd", hidden, cot_blk, precision=HIGH).reshape(count, -1)
     grecv = exchange(jnp.concatenate([d_gu, d_dn], axis=1))
     grecv = grecv.reshape(zcount, group, -1).sum(axis=0)

time: 277 us -> 276 us (level)
  waiting for transfers between devices: 107 us -> 112 us
    all_to_all x7, waiting for transfers between devices: 83 us -> 87.9 us  [exchange(): return lax.all_to_all(x, axis, 0, 0, tiled=True)]
    unnamed x59 -> x55, local copies, waits for them, and re-layouts: 11.7 us -> 8.69 us
    dot_general x6 -> x3, matrix products: 10.2 us -> 10.1 us  [the longest x1 5.07 us: per_device(): jnp.einsum('tnd,gtnf->dgnf', x_blk, grad_both, precision=HIGH)]
  transfers between devices with their start and end apart: 17 -> 17, of which waited for: 10 -> 11; matrix products, arithmetic and copies ran while one was open for 20% -> 18% of each run, Pallas kernels for 0% -> 0%
where the time goes in v2:
time: 276 us; the launch traced here: 275 us
  waiting for transfers between devices  112 us (41%)
  starting transfers between devices  88 us (32%)
  local copies, waits for them, and re-layouts  32.4 us (12%)
  matrix products  22.6 us (8%)
  other arithmetic  19.2 us (7%)
    all_to_all x7, waiting for transfers between devices, exchange(): return lax.all_to_all(x, axis, 0, 0, tiled=True)  87.9 us
    all_to_all x7, starting transfers between devices, exchange(): return lax.all_to_all(x, axis, 0, 0, tiled=True)  48.9 us
    ppermute x10, starting transfers between devices, from_partner(): return lax.ppermute(block, axis, route)  39 us
    ppermute x10, waiting for transfers between devices, from_partner(): return lax.ppermute(block, axis, route)  23.7 us
    unnamed x55, local copies, waits for them, and re-layouts  8.69 us
    all_to_all x5, local copies, waits for them, and re-layouts, exchange(): return lax.all_to_all(x, axis, 0, 0, tiled=True)  8.08 us
    reduce_sum x2, other arithmetic, backward_section(): jnp.sum(grad * field, axis=0)  5.55 us
  transfers between devices with their start and end apart: 17, of which 11 were waited for; matrix products, arithmetic and copies ran while one was open for 18% of the time, Pallas kernels for 0%

profile of v2, /device:TPU:1, one launch (start us, length us, event | category | flops | bytes accessed | tf_op | source)
XLA Modules:
  0.0 275.0 jit_solution(8921410750870818438)
XLA Ops:
  0.6 7.8 %collective-permute-start = (f32[1,128,2048]{2,1,0:T(8,128)}, f32[1,128,2048]{2,1,0:T(8,128)S(1)}, u32[]{:S(2)}, u32[]{:S(2)}) collective-permute-start(f32[1,128,2048]{2,1,0:T(8,128)} %param.8), channel_id=1, source_target_pairs={{0,16},{16,0},{1,17},{17,1},{2,18},{18,2},{3,19},{19,3},{4,20},{20... | collective-permute-start | bytes 3145736 | tf_op jit(solution)/shard_map/ppermute | solution.py:30
  8.5 1.5 copy.120
  11.0 1.4 copy.125
  12.4 5.6 %all-to-all-start.1 = ((f32[8,128,2,128]{3,1,2,0:T(8,128)}), f32[8,128,2,128]{3,1,2,0:T(8,128)S(1)}, u32[]{:S(2)}, u32[]{:S(2)}) async-start(f32[8,128,2,128]{3,1,2,0:T(8,128)} %copy.125), calls=%async_computation.1 | async-start | bytes 2097152 | tf_op jit(solution)/shard_map/all_to_all | solution.py:63
  20.1 16.9 %collective-permute-done = f32[1,128,2048]{2,1,0:T(8,128)S(1)} collective-permute-done((f32[1,128,2048]{2,1,0:T(8,128)}, f32[1,128,2048]{2,1,0:T(8,128)S(1)}, u32[]{:S(2)}, u32[]{:S(2)}) %collective-permute-start) | collective-permute-done | bytes 1048608 | tf_op jit(solution)/shard_map/ppermute | solution.py:30
  38.0 3.3 %multiply_add_fusion.1 = (f32[128,2048]{0,1:T(8,128)S(1)}, f32[128,2048]{0,1:T(8,128)}) fusion(f32[128,2048]{0,1:T(8,128)S(1)} %convolution_bitcast_fusion.2, f32[2048]{0:T(1024)S(1)} %bitcast.187, f32[2048]{0:T(1024)S(1)} %bitcast.182, f32[128,128]{1,0:T(8,128)S(1)} %copy-done, f32[1,128,2048]{2,1,0:T(8,128)} %copy-done.13), kind=kOutput, calls=%fused_computation.48 | convolution fusion | flops 202113024 | bytes 4276224 | tf_op jit(solution)/shard_map/ij,kjd->kid/dot_general | solution.py:103
  41.2 17.1 %collective-permute-start.1 = (f32[128,2048]{0,1:T(8,128)S(1)}, f32[128,2048]{0,1:T(8,128)}, u32[]{:S(2)}, u32[]{:S(2)}) collective-permute-start(f32[128,2048]{0,1:T(8,128)S(1)} %get-tuple-element.74), channel_id=1, source_target_pairs={{0,1},{1,0},{2,3},{3,2},{4,5},{5,4},{6,7},{7,6},{8,9},{9,8},{10,11... | collective-permute-start | bytes 3145736 | tf_op jit(solution)/shard_map/ppermute | solution.py:30
  59.3 3.0 %all_to_all.33 = f32[32,1,6144]{2,1,0:T(1,128)} reshape(f32[4,8,6144]{2,1,0:T(8,128)} %broadcast_in_dim.6) | data formatting | bytes 1572864 | tf_op jit(solution)/shard_map/all_to_all | solution.py:63
  62.3 10.6 %all-to-all-start = ((f32[32,1,6144]{2,1,0:T(1,128)}), f32[32,1,6144]{2,1,0:T(1,128)}, u32[]{:S(2)}, u32[]{:S(2)}) async-start(f32[32,1,6144]{2,1,0:T(1,128)} %all_to_all.33), calls=%async_computation | async-start | bytes 1572864 | tf_op jit(solution)/shard_map/all_to_all | solution.py:63
  72.9 1.4 copy.121
  74.3 1.9 multiply_reduce_fusion.5
  76.2 1.4 multiply_multiply_fusion
  77.6 15.4 %all-to-all-done = f32[32,1,6144]{2,1,0:T(1,128)} async-done(((f32[32,1,6144]{2,1,0:T(1,128)}), f32[32,1,6144]{2,1,0:T(1,128)}, u32[]{:S(2)}, u32[]{:S(2)}) %all-to-all-start) | async-done | bytes 786464 | tf_op jit(solution)/shard_map/all_to_all | solution.py:63
  92.9 8.1 %all-to-all-start.2 = ((f32[8,128,2,128]{1,3,2,0:T(8,128)}), f32[8,128,2,128]{1,3,2,0:T(8,128)}, u32[]{:S(2)}, u32[]{:S(2)}) async-start(f32[8,128,2,128]{1,3,2,0:T(8,128)} %bitcast.21), calls=%async_computation.2 | async-start | bytes 2097152 | tf_op jit(solution)/shard_map/all_to_all | solution.py:63
  103.1 1.4 copy.178
  104.6 1.2 reshape.193
  106.0 10.2 %all-to-all-done.2 = f32[8,128,2,128]{1,3,2,0:T(8,128)} async-done(((f32[8,128,2,128]{1,3,2,0:T(8,128)}), f32[8,128,2,128]{1,3,2,0:T(8,128)}, u32[]{:S(2)}, u32[]{:S(2)}) %all-to-all-start.2) | async-done | bytes 1048608 | tf_op jit(solution)/shard_map/all_to_all | solution.py:63
  116.3 1.6 copy.128
  117.8 3.3 %convolution_bitcast_fusion.3 = f32[2,1024,2,256]{1,3,2,0:T(8,128)S(1)} fusion(f32[1024,2,128,1]{2,0,1,3:T(8,128)S(1)} %bitcast.166, f32[128,2,2,256]{3,2,1,0:T(2,128)} %reshape.193), kind=kOutput, calls=%fused_computation.10 | convolution fusion | flops 805306368 | bytes 5767168 | tf_op jit(solution)/shard_map/tnd,dgnf->gtnf/dot_general | solution.py:113
  121.2 2.2 fusion.19
  123.4 1.8 fusion.8
  125.3 1.7 fusion.13
  128.3 4.3 %all-to-all-start.3 = ((f32[8,128,2,128]{1,3,2,0:T(8,128)}), f32[8,128,2,128]{1,3,2,0:T(8,128)S(1)}, u32[]{:S(2)}, u32[]{:S(2)}) async-start(f32[8,128,2,128]{1,3,2,0:T(8,128)} %bitcast.168), calls=%async_computation.3 | async-start | bytes 2097152 | tf_op jit(solution)/shard_map/all_to_all | solution.py:63
  132.7 5.1 %fusion.16 = f32[128,2,2,256]{0,3,1,2:T(8,128)} fusion(f32[1024,2,128,1]{2,0,3,1:T(8,128)} %bitcast.167, f32[1,1024,2,256]{1,3,2,0:T(8,128)} %copy-done.8, f32[1,1024,2,256]{1,3,2,0:T(8,128)} %copy-done.7), kind=kOutput, calls=%fused_computation.24 | convolution fusion | flops 806354944 | bytes 5767168 | tf_op jit(solution)/shard_map/tnd,gtnf->dgnf/dot_general | solution.py:125
  137.7 2.1 copy.135
  139.8 2.3 reshape.201
  145.3 1.7 copy.137
  147.8 5.3 %all-to-all-start.4 = ((f32[32,1,6144]{2,1,0:T(1,128)}), f32[32,1,6144]{2,1,0:T(1,128)}, u32[]{:S(2)}, u32[]{:S(2)}) async-start(f32[32,1,6144]{2,1,0:T(1,128)} %copy.137), calls=%async_computation.4 | async-start | bytes 1572864 | tf_op jit(solution)/shard_map/all_to_all | solution.py:63
  153.1 1.2 fusion.25
  154.3 3.1 %multiply_reduce_fusion.1 = (f32[2048]{0:T(1024)S(1)}, f32[2048]{0:T(1024)S(1)}, f32[128,2048]{0,1:T(8,128)S(1)}) fusion(f32[128,2048]{0,1:T(8,128)} %copy-done.4, f32[128,2048]{0,1:T(8,128)} %collective-permute-done.1, f32[128]{0:T(128)S(1)} %broadcast_multiply_fusion.2, f32[128,2048]{0,1:T(8,128)S(1)} %get-tuple-element.65, f32[2048]{0:T(1024)S(1)} %copy-done.17, ...), kind=kLoop, calls=%fused_computation.41 | loop fusion | flops 3141632 | bytes 6317056 | tf_op jit(solution)/shard_map/reduce_sum | solution.py:51
  158.4 14.8 %all-to-all-done.4 = f32[32,1,6144]{2,1,0:T(1,128)} async-done(((f32[32,1,6144]{2,1,0:T(1,128)}), f32[32,1,6144]{2,1,0:T(1,128)}, u32[]{:S(2)}, u32[]{:S(2)}) %all-to-all-start.4) | async-done | bytes 786464 | tf_op jit(solution)/shard_map/all_to_all | solution.py:63
  173.3 1.4 bitcast_reduce_fusion
  175.0 5.1 %collective-permute-start.4 = (f32[49152]{0:T(1024)S(1)}, f32[49152]{0:T(1024)S(1)}, u32[]{:S(2)}, u32[]{:S(2)}) collective-permute-start(f32[49152]{0:T(1024)S(1)} %pad_maximum_fusion.2), channel_id=1, source_target_pairs={{0,32},{32,0},{64,96},{96,64},{128,160},{160,128},{192,224},{224,1... | collective-permute-start | bytes 589832 | tf_op jit(solution)/shard_map/ppermute | solution.py:30
  180.9 1.2 collective-permute-start.2
  182.1 2.5 collective-permute-done.4
  184.6 1.3 collective-permute-start.5
  185.9 2.5 multiply_reduce_fusion.3
  190.6 1.3 fusion.22
  192.8 6.3 %all-to-all-start.5 = ((f32[32,1,1088]{2,1,0:T(1,128)}), f32[32,1,1088]{2,1,0:T(1,128)S(1)}, u32[]{:S(2)}, u32[]{:S(2)}) async-start(f32[32,1,1088]{2,1,0:T(1,128)} %all_to_all.41), calls=%async_computation.5 | async-start | bytes 294912 | tf_op jit(solution)/shard_map/all_to_all | solution.py:63
  200.0 2.5 collective-permute-start.6
  202.6 8.2 %all-to-all-done.5 = f32[32,1,1088]{2,1,0:T(1,128)S(1)} async-done(((f32[32,1,1088]{2,1,0:T(1,128)}), f32[32,1,1088]{2,1,0:T(1,128)S(1)}, u32[]{:S(2)}, u32[]{:S(2)}) %all-to-all-start.5) | async-done | bytes 139296 | tf_op jit(solution)/shard_map/all_to_all | solution.py:63
  211.7 1.7 collective-permute-done.7
  214.2 1.8 collective-permute-done.8
  216.0 2.4 collective-permute-start.9
  220.7 8.8 %all-to-all-start.6 = ((f32[32,1,1088]{2,1,0:T(1,128)}), f32[32,1,1088]{2,1,0:T(1,128)S(1)}, u32[]{:S(2)}, u32[]{:S(2)}) async-start(f32[32,1,1088]{2,1,0:T(1,128)} %broadcast_in_dim.8), calls=%async_computation.6 | async-start | bytes 294912 | tf_op jit(solution)/shard_map/all_to_all | solution.py:63
  230.1 38.5 %all-to-all-done.6 = f32[32,1,1088]{2,1,0:T(1,128)S(1)} async-done(((f32[32,1,1088]{2,1,0:T(1,128)}), f32[32,1,1088]{2,1,0:T(1,128)S(1)}, u32[]{:S(2)}, u32[]{:S(2)}) %all-to-all-start.6) | async-done | bytes 139296 | tf_op jit(solution)/shard_map/all_to_all | solution.py:63
  271.7 2.0 fusion.5
  273.6 1.3 copy.141
  (118 shorter events, 26.6 us)
Async XLA Ops:
  0.6 18.5 %copy-start = (f32[128,128]{1,0:T(8,128)S(1)}, f32[128,128]{1,0:T(8,128)}, u32[]{:S(2)}) copy-start(f32[128,128]{1,0:T(8,128)} %param.10) | copy-start | bytes 196612
  0.6 36.4 %collective-permute-start = (f32[1,128,2048]{2,1,0:T(8,128)}, f32[1,128,2048]{2,1,0:T(8,128)S(1)}, u32[]{:S(2)}, u32[]{:S(2)}) collective-permute-start(f32[1,128,2048]{2,1,0:T(8,128)} %param.8), channel_id=1, source_target_pairs={{0,16},{16,0},{1,17},{17,1},{2,18},{18,2},{3,19},{19,3},{4,20},{20... | collective-permute-start | bytes 3145736 | tf_op jit(solution)/shard_map/ppermute | solution.py:30
  10.0 1.0 copy-start.3
  11.0 6.9 %copy-start.21 = (f32[8,16,128]{2,1,0:T(8,128)S(1)}, f32[8,16,128]{2,1,0:T(8,128)}, u32[]{:S(2)}) copy-start(f32[8,16,128]{2,1,0:T(8,128)} %param.15) | copy-start | bytes 196612
  11.0 7.0 %copy-start.16 = (f32[4,2,16,256]{3,2,1,0:T(8,128)S(1)}, f32[4,2,16,256]{3,2,1,0:T(8,128)}, u32[]{:S(2)}) copy-start(f32[4,2,16,256]{3,2,1,0:T(8,128)} %param.14) | copy-start | bytes 393220
  12.4 6.7 %copy-start.1 = (f32[1,128,2048]{2,1,0:T(8,128)S(1)}, f32[1,128,2048]{2,1,0:T(8,128)}, u32[]{:S(2)}) copy-start(f32[1,128,2048]{2,1,0:T(8,128)} %param.8) | copy-start | bytes 3145732
  12.4 49.9 %all-to-all-start.1 = ((f32[8,128,2,128]{3,1,2,0:T(8,128)}), f32[8,128,2,128]{3,1,2,0:T(8,128)S(1)}, u32[]{:S(2)}, u32[]{:S(2)}) async-start(f32[8,128,2,128]{3,1,2,0:T(8,128)} %copy.125), calls=%async_computation.1 | async-start | bytes 2097152 | tf_op jit(solution)/shard_map/all_to_all | solution.py:63
  19.1 55.1 %copy-start.18 = (f32[1,1,2048]{2,1,0:T(1,128)}, f32[1,1,2048]{2,1,0:T(1,128)S(1)}, u32[]{:S(2)}) copy-start(f32[1,1,2048]{2,1,0:T(1,128)S(1)} %get-tuple-element.70) | copy-start | bytes 24580
  19.1 55.1 %copy-start.19 = (f32[1,1,2048]{2,1,0:T(1,128)}, f32[1,1,2048]{2,1,0:T(1,128)S(1)}, u32[]{:S(2)}) copy-start(f32[1,1,2048]{2,1,0:T(1,128)S(1)} %get-tuple-element.71) | copy-start | bytes 24580
  20.1 21.1 %copy-start.2 = (f32[128,2048]{0,1:T(8,128)}, f32[128,2048]{0,1:T(8,128)S(1)}, u32[]{:S(2)}) copy-start(f32[128,2048]{0,1:T(8,128)S(1)} %convolution_bitcast_fusion.2) | copy-start | bytes 3145732
  37.0 1.0 copy-start.13
  41.2 33.0 %copy-start.4 = (f32[128,2048]{0,1:T(8,128)}, f32[128,2048]{0,1:T(8,128)S(1)}, u32[]{:S(2)}) copy-start(f32[128,2048]{0,1:T(8,128)S(1)} %get-tuple-element.74) | copy-start | bytes 3145732
  41.2 33.0 %collective-permute-start.1 = (f32[128,2048]{0,1:T(8,128)S(1)}, f32[128,2048]{0,1:T(8,128)}, u32[]{:S(2)}, u32[]{:S(2)}) collective-permute-start(f32[128,2048]{0,1:T(8,128)S(1)} %get-tuple-element.74), channel_id=1, source_target_pairs={{0,1},{1,0},{2,3},{3,2},{4,5},{5,4},{6,7},{7,6},{8,9},{9,8},{10,11... | collective-permute-start | bytes 3145736 | tf_op jit(solution)/shard_map/ppermute | solution.py:30
  62.3 11.9 %copy-start.10 = (f32[8,128,2,128]{3,1,2,0:T(8,128)}, f32[8,128,2,128]{3,1,2,0:T(8,128)S(1)}, u32[]{:S(2)}) copy-start(f32[8,128,2,128]{3,1,2,0:T(8,128)S(1)} %all-to-all-done.1) | copy-start | bytes 3145732
  62.3 30.6 %all-to-all-start = ((f32[32,1,6144]{2,1,0:T(1,128)}), f32[32,1,6144]{2,1,0:T(1,128)}, u32[]{:S(2)}, u32[]{:S(2)}) async-start(f32[32,1,6144]{2,1,0:T(1,128)} %all_to_all.33), calls=%async_computation | async-start | bytes 1572864 | tf_op jit(solution)/shard_map/all_to_all | solution.py:63
  74.3 2.0 copy-start.17
  76.2 25.9 %copy-start.11 = (f32[8,128,2,128]{3,1,2,0:T(8,128)S(1)}, f32[8,128,2,128]{3,1,2,0:T(8,128)}, u32[]{:S(2)}) copy-start(f32[8,128,2,128]{3,1,2,0:T(8,128)} %copy-done.10) | copy-start | bytes 3145732
  92.9 23.3 %all-to-all-start.2 = ((f32[8,128,2,128]{1,3,2,0:T(8,128)}), f32[8,128,2,128]{1,3,2,0:T(8,128)}, u32[]{:S(2)}, u32[]{:S(2)}) async-start(f32[8,128,2,128]{1,3,2,0:T(8,128)} %bitcast.21), calls=%async_computation.2 | async-start | bytes 2097152 | tf_op jit(solution)/shard_map/all_to_all | solution.py:63
  117.8 3.4 %copy-start.6 = (f32[8,128,2,128]{3,1,0,2:T(8,128)}, f32[8,128,2,128]{3,1,0,2:T(8,128)S(1)}, u32[]{:S(2)}) copy-start(f32[8,128,2,128]{3,1,0,2:T(8,128)S(1)} %copy.128) | copy-start | bytes 3145732
  117.8 3.4 %copy-start.15 = (f32[8,128,2,128]{3,1,0,2:T(8,128)S(1)}, f32[8,128,2,128]{3,1,0,2:T(8,128)}, u32[]{:S(2)}) copy-start(f32[8,128,2,128]{3,1,0,2:T(8,128)} %copy.126) | copy-start | bytes 3145732
  123.4 1.9 copy-start.9
  125.2 1.7 copy-start.7
  125.2 2.0 copy-start.8
  128.3 19.4 %all-to-all-start.3 = ((f32[8,128,2,128]{1,3,2,0:T(8,128)}), f32[8,128,2,128]{1,3,2,0:T(8,128)S(1)}, u32[]{:S(2)}, u32[]{:S(2)}) async-start(f32[8,128,2,128]{1,3,2,0:T(8,128)} %bitcast.168), calls=%async_computation.3 | async-start | bytes 2097152 | tf_op jit(solution)/shard_map/all_to_all | solution.py:63
  147.8 6.6 %copy-start.5 = (f32[8,128,2,128]{1,3,2,0:T(8,128)}, f32[8,128,2,128]{1,3,2,0:T(8,128)S(1)}, u32[]{:S(2)}) copy-start(f32[8,128,2,128]{1,3,2,0:T(8,128)S(1)} %all-to-all-done.3) | copy-start | bytes 3145732
  147.8 25.5 %all-to-all-start.4 = ((f32[32,1,6144]{2,1,0:T(1,128)}), f32[32,1,6144]{2,1,0:T(1,128)}, u32[]{:S(2)}, u32[]{:S(2)}) async-start(f32[32,1,6144]{2,1,0:T(1,128)} %copy.137), calls=%async_computation.4 | async-start | bytes 1572864 | tf_op jit(solution)/shard_map/all_to_all | solution.py:63
  154.3 3.7 %copy-start.20 = (f32[1,1,2048]{2,1,0:T(1,128)S(1)}, f32[1,1,2048]{2,1,0:T(1,128)}, u32[]{:S(2)}) copy-start(f32[1,1,2048]{2,1,0:T(1,128)} %copy-done.19) | copy-start | bytes 24580
  175.0 9.5 %collective-permute-start.4 = (f32[49152]{0:T(1024)S(1)}, f32[49152]{0:T(1024)S(1)}, u32[]{:S(2)}, u32[]{:S(2)}) collective-permute-start(f32[49152]{0:T(1024)S(1)} %pad_maximum_fusion.2), channel_id=1, source_target_pairs={{0,32},{32,0},{64,96},{96,64},{128,160},{160,128},{192,224},{224,1... | collective-permute-start | bytes 589832 | tf_op jit(solution)/shard_map/ppermute | solution.py:30
  180.9 5.0 %collective-permute-start.2 = (f32[128,2048]{0,1:T(8,128)S(1)}, f32[128,2048]{0,1:T(8,128)S(1)}, u32[]{:S(2)}, u32[]{:S(2)}) collective-permute-start(f32[128,2048]{0,1:T(8,128)S(1)} %broadcast_multiply_fusion), channel_id=1, source_target_pairs={{0,1},{1,0},{2,3},{3,2},{4,5},{5,4},{6,7},{7,6},{8,9},{9,8},{10,11... | collective-permute-start | bytes 3145736 | tf_op jit(solution)/shard_map/ppermute | solution.py:30
  184.6 14.5 %collective-permute-start.5 = (f32[49152]{0:T(1024)S(1)}, f32[49152]{0:T(1024)}, u32[]{:S(2)}, u32[]{:S(2)}) collective-permute-start(f32[49152]{0:T(1024)S(1)} %fusion.41), channel_id=1, source_target_pairs={{0,64},{64,0},{32,96},{96,32},{128,192},{192,128},{160,224},{224,1... | collective-permute-start | bytes 589832 | tf_op jit(solution)/shard_map/ppermute | solution.py:30
  185.9 2.5 copy-start.23
  188.4 1.2 copy-start.14
  189.6 2.3 copy-start.12
  189.6 2.3 copy-start.22
  192.8 18.0 %all-to-all-start.5 = ((f32[32,1,1088]{2,1,0:T(1,128)}), f32[32,1,1088]{2,1,0:T(1,128)S(1)}, u32[]{:S(2)}, u32[]{:S(2)}) async-start(f32[32,1,1088]{2,1,0:T(1,128)} %all_to_all.41), calls=%async_computation.5 | async-start | bytes 294912 | tf_op jit(solution)/shard_map/all_to_all | solution.py:63
  200.0 14.1 %collective-permute-start.6 = (f32[49152]{0:T(1024)S(1)}, f32[49152]{0:T(1024)S(1)}, u32[]{:S(2)}, u32[]{:S(2)}) collective-permute-start(f32[49152]{0:T(1024)S(1)} %add.101), channel_id=1, source_target_pairs={{0,128},{128,0},{32,160},{160,32},{64,192},{192,64},{96,224},{224,... | collective-permute-start | bytes 589832 | tf_op jit(solution)/shard_map/ppermute | solution.py:30
  210.9 2.6 collective-permute-start.7
  213.4 2.5 collective-permute-start.8
  213.7 58.0 %collective-permute-start.3 = (f32[128,2048]{0,1:T(8,128)}, f32[128,2048]{0,1:T(8,128)}, u32[]{:S(2)}, u32[]{:S(2)}) collective-permute-start(f32[128,2048]{0,1:T(8,128)} %copy-done.12), channel_id=1, source_target_pairs={{0,16},{16,0},{1,17},{17,1},{2,18},{18,2},{3,19},{19,3},{4,20},{20... | collective-permute-start | bytes 3145736 | tf_op jit(solution)/shard_map/ppermute | solution.py:30
  216.0 4.0 %collective-permute-start.9 = (f32[1088]{0:T(1024)S(1)}, f32[1088]{0:T(1024)S(1)}, u32[]{:S(2)}, u32[]{:S(2)}) collective-permute-start(f32[1088]{0:T(1024)S(1)} %add.105), channel_id=1, source_target_pairs={{0,128},{128,0},{32,160},{160,32},{64,192},{192,64},{96,224},{224,... | collective-permute-start | bytes 13064 | tf_op jit(solution)/shard_map/ppermute | solution.py:30
  220.7 47.9 %all-to-all-start.6 = ((f32[32,1,1088]{2,1,0:T(1,128)}), f32[32,1,1088]{2,1,0:T(1,128)S(1)}, u32[]{:S(2)}, u32[]{:S(2)}) async-start(f32[32,1,1088]{2,1,0:T(1,128)} %broadcast_in_dim.8), calls=%async_computation.6 | async-start | bytes 294912 | tf_op jit(solution)/shard_map/all_to_all | solution.py:63

commit v3 on v2

--- a/solution.py
+++ b/solution.py
@@ -99,8 +99,9 @@
 
     xb = seq_in.reshape(nblocks, BLK, width)
     xb_peer = from_partner(xb, SEQ, top_bit)
-    mixed = jnp.einsum("ij,kjd->kid", block_mix, xb, precision=HIGH).reshape(tokens, width)
-    mixed_peer = jnp.einsum("ij,kjd->kid", block_mix, xb_peer, precision=HIGH).reshape(tokens, width)
+    mixed_both = jnp.einsum("ij,kjd->kid", block_mix, jnp.concatenate([xb, xb_peer]), precision=HIGH)
+    mixed = mixed_both[:nblocks].reshape(tokens, width)
+    mixed_peer = mixed_both[nblocks:].reshape(tokens, width)
     own_hi = twist_hi[side_of(top_bit)]
     first = own_hi[0] * mixed + own_hi[1] * mixed_peer
     second, first_peer = forward_section(first, twist_lo, 0)
@@ -144,8 +145,8 @@
     grad_mb = grad_mixed.reshape(nblocks, BLK, width)
     keep = (own_hi[0] * grad_first).reshape(nblocks, BLK, width)
     give = (own_hi[1] * grad_first).reshape(nblocks, BLK, width)
-    term_block = jnp.einsum("kid,kjd->ij", keep, xb, precision=HIGH) + jnp.einsum(
-        "kid,kjd->ij", give, xb_peer, precision=HIGH
+    term_block = jnp.einsum(
+        "kid,kjd->ij", jnp.concatenate([keep, give]), jnp.concatenate([xb, xb_peer]), precision=HIGH
     )
     grad_seq = jnp.einsum("ij,kid->kjd", block_mix, grad_mb, precision=HIGH).reshape(tokens, width)
     grad_seq = grad_seq + grad_resid

time: 276 us -> 279 us (1.011)
  other arithmetic: 19.2 us -> 23.4 us
  waiting for transfers between devices: 112 us -> 109 us
    all_to_all x7, waiting for transfers between devices: 87.9 us -> 80.9 us  [exchange(): return lax.all_to_all(x, axis, 0, 0, tiled=True)]
    ppermute x10, waiting for transfers between devices: 23.7 us -> 27.7 us  [from_partner(): return lax.ppermute(block, axis, route)]
    unnamed x55 -> x59, local copies, waits for them, and re-layouts: 8.69 us -> 6.88 us
    dot_general x4 -> x2, matrix products: 6.56 us -> 5.34 us  [the longest x1 3.12 us: per_device(): jnp.einsum('kid,kjd->ij', jnp.concatenate([keep, give]), jnp.concatenate(...]
  transfers between devices with their start and end apart: 17 -> 17, of which waited for: 11 -> 11; matrix products, arithmetic and copies ran while one was open for 18% -> 19% of each run, Pallas kernels for 0% -> 0%
where the time goes in v3:
time: 279 us; the launch traced here: 278 us
  waiting for transfers between devices  109 us (39%)
  starting transfers between devices  88.5 us (32%)
  local copies, waits for them, and re-layouts  34.7 us (12%)
  other arithmetic  23.4 us (8%)
  matrix products  21.4 us (8%)
    all_to_all x7, waiting for transfers between devices, exchange(): return lax.all_to_all(x, axis, 0, 0, tiled=True)  80.9 us
    all_to_all x7, starting transfers between devices, exchange(): return lax.all_to_all(x, axis, 0, 0, tiled=True)  49.7 us
    ppermute x10, starting transfers between devices, from_partner(): return lax.ppermute(block, axis, route)  38.8 us
    ppermute x10, waiting for transfers between devices, from_partner(): return lax.ppermute(block, axis, route)  27.7 us
    all_to_all x5, local copies, waits for them, and re-layouts, exchange(): return lax.all_to_all(x, axis, 0, 0, tiled=True)  10.5 us
    unnamed x59, local copies, waits for them, and re-layouts  6.88 us
  transfers between devices with their start and end apart: 17, of which 11 were waited for; matrix products, arithmetic and copies ran while one was open for 19% of the time, Pallas kernels for 0%

profile of v3, /device:TPU:1, one launch (start us, length us, event | category | flops | bytes accessed | tf_op | source)
XLA Modules:
  0.0 277.9 jit_solution(1909700033641699557)
XLA Ops:
  0.7 1.6 copy.145
  2.3 7.8 %collective-permute-start = (f32[1,128,2048]{1,2,0:T(8,128)S(1)}, f32[1,128,2048]{1,2,0:T(8,128)}, u32[]{:S(2)}, u32[]{:S(2)}) collective-permute-start(f32[1,128,2048]{1,2,0:T(8,128)S(1)} %copy.145), channel_id=1, source_target_pairs={{0,16},{16,0},{1,17},{17,1},{2,18},{18,2},{3,19},{19,3},{4,20},{20... | collective-permute-start | bytes 3145736 | tf_op jit(solution)/shard_map/ppermute | solution.py:30
  10.5 1.3 copy.151
  11.8 5.6 %all-to-all-start.1 = ((f32[8,128,2,128]{3,1,2,0:T(8,128)}), f32[8,128,2,128]{3,1,2,0:T(8,128)}, u32[]{:S(2)}, u32[]{:S(2)}) async-start(f32[8,128,2,128]{3,1,2,0:T(8,128)} %copy.151), calls=%async_computation.1 | async-start | bytes 2097152 | tf_op jit(solution)/shard_map/all_to_all | solution.py:63
  17.8 20.8 %collective-permute-done = f32[1,128,2048]{1,2,0:T(8,128)} collective-permute-done((f32[1,128,2048]{1,2,0:T(8,128)S(1)}, f32[1,128,2048]{1,2,0:T(8,128)}, u32[]{:S(2)}, u32[]{:S(2)}) %collective-permute-start) | collective-permute-done | bytes 1048608 | tf_op jit(solution)/shard_map/ppermute | solution.py:30
  38.6 2.2 convolution_bitcast_fusion
  40.8 1.5 multiply_add_fusion.1
  42.3 16.9 %collective-permute-start.1 = (f32[128,2048]{0,1:T(8,128)}, f32[128,2048]{0,1:T(8,128)S(1)}, u32[]{:S(2)}, u32[]{:S(2)}) collective-permute-start(f32[128,2048]{0,1:T(8,128)} %multiply_add_fusion.1), channel_id=1, source_target_pairs={{0,1},{1,0},{2,3},{3,2},{4,5},{5,4},{6,7},{7,6},{8,9},{9,8},{10,11... | collective-permute-start | bytes 3145736 | tf_op jit(solution)/shard_map/ppermute | solution.py:30
  60.2 3.0 %all_to_all.33 = f32[32,1,6144]{2,1,0:T(1,128)} reshape(f32[4,8,6144]{2,1,0:T(8,128)} %broadcast_in_dim.6) | data formatting | bytes 1572864 | tf_op jit(solution)/shard_map/all_to_all | solution.py:63
  63.1 10.7 %all-to-all-start = ((f32[32,1,6144]{2,1,0:T(1,128)}), f32[32,1,6144]{2,1,0:T(1,128)}, u32[]{:S(2)}, u32[]{:S(2)}) async-start(f32[32,1,6144]{2,1,0:T(1,128)} %all_to_all.33), calls=%async_computation | async-start | bytes 1572864 | tf_op jit(solution)/shard_map/all_to_all | solution.py:63
  74.9 3.2 %multiply_reduce_fusion.5 = (f32[128]{0:T(128)S(1)}, f32[128,2048]{0,1:T(8,128)S(1)}) fusion(f32[128,2048]{0,1:T(8,128)} %copy-done.12, f32[2048]{0:T(1024)S(1)} %bitcast.199, f32[2048]{0:T(1024)S(1)} %bitcast.197, f32[1,128,2048]{1,2,0:T(8,128)} %copy-done.3, f32[2,128,2048]{1,2,0:T(8,128)S(1)} %convolution_bitcast_fusion, f32[2048]{0:T(1024)S(1)} %bitcast.192, ...), kind=kLoop, calls=%fused_computation.46 | loop fusion | flops 2359168 | bytes 5276160 | tf_op jit(solution)/shard_map/reduce_sum | solution.py:109
  79.4 14.6 %all-to-all-done = f32[32,1,6144]{2,1,0:T(1,128)} async-done(((f32[32,1,6144]{2,1,0:T(1,128)}), f32[32,1,6144]{2,1,0:T(1,128)}, u32[]{:S(2)}, u32[]{:S(2)}) %all-to-all-start) | async-done | bytes 786464 | tf_op jit(solution)/shard_map/all_to_all | solution.py:63
  94.0 8.1 %all-to-all-start.2 = ((f32[8,128,2,128]{1,3,2,0:T(8,128)}), f32[8,128,2,128]{1,3,2,0:T(8,128)}, u32[]{:S(2)}, u32[]{:S(2)}) async-start(f32[8,128,2,128]{1,3,2,0:T(8,128)} %bitcast.170), calls=%async_computation.2 | async-start | bytes 2097152 | tf_op jit(solution)/shard_map/all_to_all | solution.py:63
  103.1 2.4 copy.152
  105.5 1.4 copy.208
  107.8 2.3 reshape.184
  111.0 6.3 %all-to-all-done.2 = f32[8,128,2,128]{1,3,2,0:T(8,128)} async-done(((f32[8,128,2,128]{1,3,2,0:T(8,128)}), f32[8,128,2,128]{1,3,2,0:T(8,128)}, u32[]{:S(2)}, u32[]{:S(2)}) %all-to-all-start.2) | async-done | bytes 1048608 | tf_op jit(solution)/shard_map/all_to_all | solution.py:63
  117.3 2.6 copy.154
  119.9 3.4 %convolution_bitcast_fusion.3 = f32[2,1024,2,256]{1,3,2,0:T(8,128)S(1)} fusion(f32[1024,2,128,1]{2,0,1,3:T(8,128)} %bitcast.168, f32[128,2,2,256]{3,2,1,0:T(2,128)} %reshape.184), kind=kOutput, calls=%fused_computation.10 | convolution fusion | flops 805306368 | bytes 5767168 | tf_op jit(solution)/shard_map/tnd,dgnf->gtnf/dot_general | solution.py:114
  123.3 2.2 fusion.22
  125.4 1.8 fusion.11
  127.3 1.7 fusion.16
  130.4 5.0 %all-to-all-start.3 = ((f32[8,128,2,128]{1,3,2,0:T(8,128)}), f32[8,128,2,128]{1,3,2,0:T(8,128)}, u32[]{:S(2)}, u32[]{:S(2)}) async-start(f32[8,128,2,128]{1,3,2,0:T(8,128)} %bitcast.171), calls=%async_computation.3 | async-start | bytes 2097152 | tf_op jit(solution)/shard_map/all_to_all | solution.py:63
  135.4 5.1 %fusion.19 = f32[128,2,2,256]{0,3,1,2:T(8,128)} fusion(f32[1024,2,128,1]{2,0,3,1:T(8,128)} %bitcast.169, f32[1,1024,2,256]{1,3,2,0:T(8,128)} %copy-done.10, f32[1,1024,2,256]{1,3,2,0:T(8,128)} %copy-done.9), kind=kOutput, calls=%fused_computation.28 | convolution fusion | flops 806354944 | bytes 5767168 | tf_op jit(solution)/shard_map/tnd,gtnf->dgnf/dot_general | solution.py:126
  140.5 2.0 copy.161
  142.5 2.3 reshape.192
  148.1 1.7 copy.163
  150.6 5.3 %all-to-all-start.4 = ((f32[32,1,6144]{2,1,0:T(1,128)}), f32[32,1,6144]{2,1,0:T(1,128)}, u32[]{:S(2)}, u32[]{:S(2)}) async-start(f32[32,1,6144]{2,1,0:T(1,128)} %copy.163), calls=%async_computation.4 | async-start | bytes 1572864 | tf_op jit(solution)/shard_map/all_to_all | solution.py:63
  156.0 2.6 fusion.25
  158.6 2.6 multiply_reduce_fusion.1
  162.2 1.3 broadcast_multiply_fusion
  163.5 12.6 %all-to-all-done.4 = f32[32,1,6144]{2,1,0:T(1,128)} async-done(((f32[32,1,6144]{2,1,0:T(1,128)}), f32[32,1,6144]{2,1,0:T(1,128)}, u32[]{:S(2)}, u32[]{:S(2)}) %all-to-all-start.4) | async-done | bytes 786464 | tf_op jit(solution)/shard_map/all_to_all | solution.py:63
  176.1 1.4 bitcast_reduce_fusion
  177.9 5.1 %collective-permute-start.4 = (f32[49152]{0:T(1024)S(1)}, f32[49152]{0:T(1024)S(1)}, u32[]{:S(2)}, u32[]{:S(2)}) collective-permute-start(f32[49152]{0:T(1024)S(1)} %pad_maximum_fusion.5), channel_id=1, source_target_pairs={{0,32},{32,0},{64,96},{96,64},{128,160},{160,128},{192,224},{224,1... | collective-permute-start | bytes 589832 | tf_op jit(solution)/shard_map/ppermute | solution.py:30
  184.9 2.5 collective-permute-done.4
  187.5 1.3 collective-permute-start.5
  188.8 1.3 multiply_bitcast_fusion
  191.7 3.1 %convolution_bitcast_fusion.2 = f32[16384]{0:T(1024)S(1)} fusion(f32[1,128,2048]{1,2,0:T(8,128)S(1)} %bitcast.172, f32[1,128,2048]{1,2,0:T(8,128)S(1)} %get-tuple-element.62, f32[1,128,2048]{1,2,0:T(8,128)} %collective-permute-done, f32[1,128,2048]{1,2,0:T(8,128)S(1)} %copy-done.4), kind=kOutput, calls=%fused_computation.9 | convolution fusion | flops 403701760 | bytes 4259840 | tf_op jit(solution)/shard_map/kid,kjd->ij/dot_general | solution.py:148
  195.7 6.3 %all-to-all-start.5 = ((f32[32,1,1088]{2,1,0:T(1,128)}), f32[32,1,1088]{2,1,0:T(1,128)S(1)}, u32[]{:S(2)}, u32[]{:S(2)}) async-start(f32[32,1,1088]{2,1,0:T(1,128)} %all_to_all.41), calls=%async_computation.5 | async-start | bytes 294912 | tf_op jit(solution)/shard_map/all_to_all | solution.py:63
  203.0 2.5 collective-permute-start.6
  205.5 8.2 %all-to-all-done.5 = f32[32,1,1088]{2,1,0:T(1,128)S(1)} async-done(((f32[32,1,1088]{2,1,0:T(1,128)}), f32[32,1,1088]{2,1,0:T(1,128)S(1)}, u32[]{:S(2)}, u32[]{:S(2)}) %all-to-all-start.5) | async-done | bytes 139296 | tf_op jit(solution)/shard_map/all_to_all | solution.py:63
  214.7 1.7 collective-permute-done.7
  217.1 1.8 collective-permute-done.8
  218.9 2.4 collective-permute-start.9
  223.7 8.8 %all-to-all-start.6 = ((f32[32,1,1088]{2,1,0:T(1,128)}), f32[32,1,1088]{2,1,0:T(1,128)S(1)}, u32[]{:S(2)}, u32[]{:S(2)}) async-start(f32[32,1,1088]{2,1,0:T(1,128)} %broadcast_in_dim.8), calls=%async_computation.6 | async-start | bytes 294912 | tf_op jit(solution)/shard_map/all_to_all | solution.py:63
  233.1 38.4 %all-to-all-done.6 = f32[32,1,1088]{2,1,0:T(1,128)S(1)} async-done(((f32[32,1,1088]{2,1,0:T(1,128)}), f32[32,1,1088]{2,1,0:T(1,128)S(1)}, u32[]{:S(2)}, u32[]{:S(2)}) %all-to-all-start.6) | async-done | bytes 139296 | tf_op jit(solution)/shard_map/all_to_all | solution.py:63
  274.6 2.0 fusion.5
  276.6 1.3 copy.169
  (121 shorter events, 26.7 us)
Async XLA Ops:
  0.6 37.9 %copy-start = (f32[128,128]{1,0:T(8,128)S(1)}, f32[128,128]{1,0:T(8,128)}, u32[]{:S(2)}) copy-start(f32[128,128]{1,0:T(8,128)} %param.10) | copy-start | bytes 196612
  0.6 9.5 %copy-start.15 = (f32[1,128,2048]{2,1,0:T(8,128)S(1)}, f32[1,128,2048]{2,1,0:T(8,128)}, u32[]{:S(2)}) copy-start(f32[1,128,2048]{2,1,0:T(8,128)} %param.9) | copy-start | bytes 3145732
  2.3 36.3 %copy-start.3 = (f32[1,128,2048]{1,2,0:T(8,128)}, f32[1,128,2048]{1,2,0:T(8,128)S(1)}, u32[]{:S(2)}) copy-start(f32[1,128,2048]{1,2,0:T(8,128)S(1)} %copy.145) | copy-start | bytes 3145732
  2.3 36.3 %collective-permute-start = (f32[1,128,2048]{1,2,0:T(8,128)S(1)}, f32[1,128,2048]{1,2,0:T(8,128)}, u32[]{:S(2)}, u32[]{:S(2)}) collective-permute-start(f32[1,128,2048]{1,2,0:T(8,128)S(1)} %copy.145), channel_id=1, source_target_pairs={{0,16},{16,0},{1,17},{17,1},{2,18},{18,2},{3,19},{19,3},{4,20},{20... | collective-permute-start | bytes 3145736 | tf_op jit(solution)/shard_map/ppermute | solution.py:30
  10.5 1.3 copy-start.5
  10.5 6.9 %copy-start.21 = (f32[8,16,128]{2,1,0:T(8,128)S(1)}, f32[8,16,128]{2,1,0:T(8,128)}, u32[]{:S(2)}) copy-start(f32[8,16,128]{2,1,0:T(8,128)} %param.15) | copy-start | bytes 196612
  10.5 7.0 %copy-start.18 = (f32[4,2,16,256]{3,2,1,0:T(8,128)S(1)}, f32[4,2,16,256]{3,2,1,0:T(8,128)}, u32[]{:S(2)}) copy-start(f32[4,2,16,256]{3,2,1,0:T(8,128)} %param.14) | copy-start | bytes 393220
  11.8 5.9 %copy-start.23 = (f32[2,2,2048]{2,1,0:T(2,128)S(1)}, f32[2,2,2048]{2,1,0:T(2,128)}, u32[]{:S(2)}) copy-start(f32[2,2,2048]{2,1,0:T(2,128)} %param.12) | copy-start | bytes 98308
  11.8 5.9 %copy-start.24 = (f32[2,2,2048]{2,1,0:T(2,128)S(1)}, f32[2,2,2048]{2,1,0:T(2,128)}, u32[]{:S(2)}) copy-start(f32[2,2,2048]{2,1,0:T(2,128)} %param.11) | copy-start | bytes 98308
  11.8 51.3 %all-to-all-start.1 = ((f32[8,128,2,128]{3,1,2,0:T(8,128)}), f32[8,128,2,128]{3,1,2,0:T(8,128)}, u32[]{:S(2)}, u32[]{:S(2)}) async-start(f32[8,128,2,128]{3,1,2,0:T(8,128)} %copy.151), calls=%async_computation.1 | async-start | bytes 2097152 | tf_op jit(solution)/shard_map/all_to_all | solution.py:63
  17.8 57.1 %copy-start.20 = (f32[1,1,2048]{2,1,0:T(1,128)}, f32[1,1,2048]{2,1,0:T(1,128)S(1)}, u32[]{:S(2)}) copy-start(f32[1,1,2048]{2,1,0:T(1,128)S(1)} %get-tuple-element.72) | copy-start | bytes 24580
  42.3 31.6 %collective-permute-start.1 = (f32[128,2048]{0,1:T(8,128)}, f32[128,2048]{0,1:T(8,128)S(1)}, u32[]{:S(2)}, u32[]{:S(2)}) collective-permute-start(f32[128,2048]{0,1:T(8,128)} %multiply_add_fusion.1), channel_id=1, source_target_pairs={{0,1},{1,0},{2,3},{3,2},{4,5},{5,4},{6,7},{7,6},{8,9},{9,8},{10,11... | collective-permute-start | bytes 3145736 | tf_op jit(solution)/shard_map/ppermute | solution.py:30
  63.1 30.9 %all-to-all-start = ((f32[32,1,6144]{2,1,0:T(1,128)}), f32[32,1,6144]{2,1,0:T(1,128)}, u32[]{:S(2)}, u32[]{:S(2)}) async-start(f32[32,1,6144]{2,1,0:T(1,128)} %all_to_all.33), calls=%async_computation | async-start | bytes 1572864 | tf_op jit(solution)/shard_map/all_to_all | solution.py:63
  73.9 1.0 copy-start.12
  74.9 3.2 %copy-start.19 = (f32[2048]{0:T(1024)S(1)}, f32[2048]{0:T(1024)}, u32[]{:S(2)}) copy-start(f32[2048]{0:T(1024)} %param.13) | copy-start | bytes 24580
  94.0 23.3 %all-to-all-start.2 = ((f32[8,128,2,128]{1,3,2,0:T(8,128)}), f32[8,128,2,128]{1,3,2,0:T(8,128)}, u32[]{:S(2)}, u32[]{:S(2)}) async-start(f32[8,128,2,128]{1,3,2,0:T(8,128)} %bitcast.170), calls=%async_computation.2 | async-start | bytes 2097152 | tf_op jit(solution)/shard_map/all_to_all | solution.py:63
  119.9 3.4 %copy-start.16 = (f32[8,128,2,128]{3,1,0,2:T(8,128)S(1)}, f32[8,128,2,128]{3,1,0,2:T(8,128)}, u32[]{:S(2)}) copy-start(f32[8,128,2,128]{3,1,0,2:T(8,128)} %copy.152) | copy-start | bytes 3145732
  123.2 2.2 copy-start.17
  125.4 1.9 copy-start.11
  127.3 1.7 copy-start.9
  127.3 2.0 copy-start.10
  130.4 20.2 %all-to-all-start.3 = ((f32[8,128,2,128]{1,3,2,0:T(8,128)}), f32[8,128,2,128]{1,3,2,0:T(8,128)}, u32[]{:S(2)}, u32[]{:S(2)}) async-start(f32[8,128,2,128]{1,3,2,0:T(8,128)} %bitcast.171), calls=%async_computation.3 | async-start | bytes 2097152 | tf_op jit(solution)/shard_map/all_to_all | solution.py:63
  150.6 25.5 %all-to-all-start.4 = ((f32[32,1,6144]{2,1,0:T(1,128)}), f32[32,1,6144]{2,1,0:T(1,128)}, u32[]{:S(2)}, u32[]{:S(2)}) async-start(f32[32,1,6144]{2,1,0:T(1,128)} %copy.163), calls=%async_computation.4 | async-start | bytes 1572864 | tf_op jit(solution)/shard_map/all_to_all | solution.py:63
  156.0 2.6 copy-start.6
  156.0 2.6 copy-start.13
  161.2 1.0 copy-start.1
  163.5 25.2 %copy-start.2 = (f32[128,2048]{0,1:T(8,128)S(1)}, f32[128,2048]{0,1:T(8,128)}, u32[]{:S(2)}) copy-start(f32[128,2048]{0,1:T(8,128)} %copy-done.1) | copy-start | bytes 3145732
  177.9 9.6 %collective-permute-start.4 = (f32[49152]{0:T(1024)S(1)}, f32[49152]{0:T(1024)S(1)}, u32[]{:S(2)}, u32[]{:S(2)}) collective-permute-start(f32[49152]{0:T(1024)S(1)} %pad_maximum_fusion.5), channel_id=1, source_target_pairs={{0,32},{32,0},{64,96},{96,64},{128,160},{160,128},{192,224},{224,1... | collective-permute-start | bytes 589832 | tf_op jit(solution)/shard_map/ppermute | solution.py:30
  183.8 5.0 %collective-permute-start.2 = (f32[128,2048]{0,1:T(8,128)}, f32[128,2048]{0,1:T(8,128)S(1)}, u32[]{:S(2)}, u32[]{:S(2)}) collective-permute-start(f32[128,2048]{0,1:T(8,128)} %broadcast_multiply_fusion), channel_id=1, source_target_pairs={{0,1},{1,0},{2,3},{3,2},{4,5},{5,4},{6,7},{7,6},{8,9},{9,8},{10,11... | collective-permute-start | bytes 3145736 | tf_op jit(solution)/shard_map/ppermute | solution.py:30
  187.5 14.6 %collective-permute-start.5 = (f32[49152]{0:T(1024)S(1)}, f32[49152]{0:T(1024)}, u32[]{:S(2)}, u32[]{:S(2)}) collective-permute-start(f32[49152]{0:T(1024)S(1)} %fusion.39), channel_id=1, source_target_pairs={{0,64},{64,0},{32,96},{96,32},{128,192},{192,128},{160,224},{224,1... | collective-permute-start | bytes 589832 | tf_op jit(solution)/shard_map/ppermute | solution.py:30
  190.1 1.0 copy-start.7
  190.1 1.0 copy-start.25
  190.1 1.6 copy-start.4
  191.1 3.7 %copy-start.14 = (f32[128,2048]{0,1:T(8,128)}, f32[128,2048]{0,1:T(8,128)S(1)}, u32[]{:S(2)}) copy-start(f32[128,2048]{0,1:T(8,128)S(1)} %get-tuple-element.69) | copy-start | bytes 3145732
  191.7 3.1 %copy-start.22 = (f32[2048]{0:T(1024)S(1)}, f32[2048]{0:T(1024)}, u32[]{:S(2)}) copy-start(f32[2048]{0:T(1024)} %get-tuple-element.58) | copy-start | bytes 24580
  195.7 78.9 %copy-start.8 = (f32[128,2048]{0,1:T(8,128)S(1)}, f32[128,2048]{0,1:T(8,128)}, u32[]{:S(2)}) copy-start(f32[128,2048]{0,1:T(8,128)} %copy-done.7) | copy-start | bytes 3145732
  195.7 18.0 %all-to-all-start.5 = ((f32[32,1,1088]{2,1,0:T(1,128)}), f32[32,1,1088]{2,1,0:T(1,128)S(1)}, u32[]{:S(2)}, u32[]{:S(2)}) async-start(f32[32,1,1088]{2,1,0:T(1,128)} %all_to_all.41), calls=%async_computation.5 | async-start | bytes 294912 | tf_op jit(solution)/shard_map/all_to_all | solution.py:63
  203.0 14.1 %collective-permute-start.6 = (f32[49152]{0:T(1024)S(1)}, f32[49152]{0:T(1024)S(1)}, u32[]{:S(2)}, u32[]{:S(2)}) collective-permute-start(f32[49152]{0:T(1024)S(1)} %add.98), channel_id=1, source_target_pairs={{0,128},{128,0},{32,160},{160,32},{64,192},{192,64},{96,224},{224,... | collective-permute-start | bytes 589832 | tf_op jit(solution)/shard_map/ppermute | solution.py:30
  213.8 2.6 collective-permute-start.7
  216.4 2.5 collective-permute-start.8
  216.7 57.9 %collective-permute-start.3 = (f32[128,2048]{0,1:T(8,128)}, f32[128,2048]{0,1:T(8,128)}, u32[]{:S(2)}, u32[]{:S(2)}) collective-permute-start(f32[128,2048]{0,1:T(8,128)} %copy-done.14), channel_id=1, source_target_pairs={{0,16},{16,0},{1,17},{17,1},{2,18},{18,2},{3,19},{19,3},{4,20},{20... | collective-permute-start | bytes 3145736 | tf_op jit(solution)/shard_map/ppermute | solution.py:30
  218.9 4.0 %collective-permute-start.9 = (f32[1088]{0:T(1024)S(1)}, f32[1088]{0:T(1024)S(1)}, u32[]{:S(2)}, u32[]{:S(2)}) collective-permute-start(f32[1088]{0:T(1024)S(1)} %add.101), channel_id=1, source_target_pairs={{0,128},{128,0},{32,160},{160,32},{64,192},{192,64},{96,224},{224,... | collective-permute-start | bytes 13064 | tf_op jit(solution)/shard_map/ppermute | solution.py:30
  223.7 47.8 %all-to-all-start.6 = ((f32[32,1,1088]{2,1,0:T(1,128)}), f32[32,1,1088]{2,1,0:T(1,128)S(1)}, u32[]{:S(2)}, u32[]{:S(2)}) async-start(f32[32,1,1088]{2,1,0:T(1,128)} %broadcast_in_dim.8), calls=%async_computation.6 | async-start | bytes 294912 | tf_op jit(solution)/shard_map/all_to_all | solution.py:63
